TPU v7x, 256 devices: a whole 4x4x8 slice. The times are simulated.
256 devices in a mesh: sta: 64 (over z, y, core), tm: 4 (over x).
Axes of the slice: x: 4, y: 4, z: 8, core: 2. Of those that a mesh axis runs over, the one named last changes fastest.
Arguments:
- records: bfloat16 [4096, 8192], P('sta', 'tm'), may hold values from -6 to 6
- band_taps: bfloat16 [1024], replicated, may hold values from -0.1875 to 0.1875
- station_owners: int32 [4096, 2], P('sta'), may hold values from 0 to 63, all different within a row; in each aligned block of 64 rows (0 to 63, 64 to 127, ...) at most 4 rows name the same one
Outputs:
- correlations: bfloat16 [4096, 2, 64, 2, 512], P('sta', None, None, None, 'tm')
Inputs may be any that keep to these rules, and one draw needn't show every extreme that they name: `station_owners`: each row names 2 different station blocks. Within the rows of one station block (64 aligned rows) no block is named by more than 4 rows, and some block is named by exactly 4 rows.
All inputs are finite; a program needn't handle non-finite values.
Results may differ from a plain program's by a relative error of at most 0.0069.
Values may be sent and summed in bfloat16 or wider, within the bound.
No kernel may reach another device: no remote copies, remote signals or barrier semaphores. Data moves between devices by JAX's collectives and lax.ppermute only.
A program may use at most 128 MiB of HBM per device.

v0:
```python
import math

import jax
import jax.numpy as jnp
from jax import lax
from jax.experimental import pallas as pl
from jax.experimental.pallas import tpu as pltpu
from jax.sharding import Mesh
from jax.sharding import PartitionSpec as P

WIN = 1024
FREQ = 512
SMOOTH = 64
NW = 8
CORES = 2


def toeplitz_kernel(seed_ref, out_ref):
    rows = 128
    base = jnp.broadcast_to(seed_ref[...], (rows, seed_ref.shape[1]))
    for blk in range(out_ref.shape[0] // rows):
        rolled = pltpu.roll(base, blk * rows, 1, stride=1, stride_axis=0)
        out_ref[blk * rows : (blk + 1) * rows, :] = rolled.astype(out_ref.dtype)


def toeplitz_both(band_taps):
    taps_len = band_taps.shape[0]
    seed = jnp.concatenate(
        [band_taps.astype(jnp.float32), jnp.zeros((taps_len,), jnp.float32)]
    )[None, :]
    return pl.pallas_call(
        toeplitz_kernel,
        out_shape=jax.ShapeDtypeStruct((taps_len, 2 * taps_len), jnp.bfloat16),
    )(seed)


def transform_table(window_len):
    bin_count = window_len // 2
    sample_index = jnp.arange(window_len, dtype=jnp.int32)[:, None]
    bin_index = jnp.arange(bin_count, dtype=jnp.int32)[None, :]
    phase_angle = (sample_index * bin_index % window_len).astype(jnp.float32) * (
        2.0 * math.pi / window_len
    )
    return jnp.concatenate([jnp.cos(phase_angle), -jnp.sin(phase_angle)], axis=1).astype(
        jnp.bfloat16
    )


def band_matrix(bin_count, smooth_len):
    bin_index = jnp.arange(bin_count, dtype=jnp.int32)
    offsets = (bin_index[:, None] - bin_index[None, :]) % bin_count
    half_span = smooth_len // 2
    inside = (offsets < half_span) | (offsets >= bin_count - half_span)
    return inside.astype(jnp.float32)


def shards(records, band_taps, station_owners):
    relayed = lax.all_to_all(records, "tm", split_axis=0, concat_axis=1, tiled=True)
    station_count = relayed.shape[0]
    both_parts = toeplitz_both(band_taps)
    series = relayed.reshape(station_count * NW, WIN)
    halves = jnp.dot(series, both_parts, preferred_element_type=jnp.float32)
    halves = halves.reshape(station_count, NW, 2 * WIN)
    carried = jnp.concatenate(
        [jnp.zeros_like(halves[:, :1, WIN:]), halves[:, :-1, WIN:]], axis=1
    )
    filtered = (halves[:, :, :WIN] + carried).astype(jnp.bfloat16).reshape(-1, WIN)
    spectrum = jnp.dot(filtered, transform_table(WIN), preferred_element_type=jnp.float32)
    real_part = spectrum[:, :FREQ]
    imag_part = spectrum[:, FREQ:]
    power_sum = real_part * real_part + imag_part * imag_part
    smooth = (
        jnp.dot(
            power_sum,
            band_matrix(FREQ, SMOOTH),
            precision=lax.Precision.HIGHEST,
            preferred_element_type=jnp.float32,
        )
        / SMOOTH
    )
    whiten_scale = lax.rsqrt(smooth + 1e-05)
    whitened = (spectrum.reshape(-1, 2, FREQ) * whiten_scale[:, None, :]).astype(jnp.bfloat16)
    whitened = whitened.reshape(station_count, NW, 2, FREQ)
    regrouped = lax.all_to_all(whitened, "tm", split_axis=3, concat_axis=0, tiled=True)
    own_count = regrouped.shape[0]
    same_core = lax.all_gather(regrouped, "zy", axis=0, tiled=False)
    both_cores = lax.all_gather(same_core, "c", axis=0, tiled=False)
    needed = both_cores[station_owners % CORES, station_owners // CORES]

    def block_sum(left_part, right_part):
        return jnp.einsum(
            "swf,skjwf->skjf", left_part, right_part, preferred_element_type=jnp.float32
        )

    sig_re = regrouped[:, :, 0]
    sig_im = regrouped[:, :, 1]
    par_re = needed[..., 0, :]
    par_im = needed[..., 1, :]
    real_sum = block_sum(sig_re, par_re) + block_sum(sig_im, par_im)
    imag_sum = block_sum(sig_im, par_re) - block_sum(sig_re, par_im)
    result = jnp.stack([real_sum, imag_sum], axis=3).astype(jnp.bfloat16)
    return result


def solution(mesh):
    n_sta, n_tm = mesh.shape["sta"], mesh.shape["tm"]
    split_mesh = Mesh(
        mesh.devices.reshape(n_sta // CORES, CORES, n_tm), ("zy", "c", "tm")
    )
    sta = ("zy", "c")
    placed = (P(sta, "tm"), P(), P(sta, None))
    return jax.shard_map(
        shards,
        mesh=split_mesh,
        in_specs=placed,
        out_specs=P(sta, None, None, None, "tm"),
        check_vma=False,
    )
```

profile of v0, /device:TPU:1, one launch (start us, length us, event | category | flops | bytes accessed | tf_op | source)
XLA Modules:
  0.0 275.5 jit_solution(10616585042823081302)
XLA Ops:
  6.5 4.8 %all-to-all-start = ((bf16[4,16,2048]{2,1,0:T(8,128)(2,1)}), bf16[4,16,2048]{2,1,0:T(8,128)(2,1)S(1)}, u32[]{:S(2)}, u32[]{:S(2)}) async-start(bf16[4,16,2048]{2,1,0:T(8,128)(2,1)} %bitcast.80), calls=%async_computation | async-start | bytes 524288 | tf_op jit(solution)/shard_map/all_to_all | solution.py:58
  11.4 1.3 pad_convert_fusion
  12.6 3.1 %shard_map.37 = bf16[1024,2048]{1,0:T(8,128)(2,1)} custom-call(f32[1,2048]{1,0:T(1,128)} %bitcast.81), custom_call_target="tpu_custom_call" | custom-call | tf_op jit(solution)/shard_map/pallas_call | solution.py:31
  15.7 8.5 %negate_convert_fusion = (bf16[1024,512]{1,0:T(8,128)(2,1)S(1)}, bf16[1024,512]{1,0:T(8,128)(2,1)S(1)}) fusion(), kind=kLoop, calls=%fused_computation.27 | loop fusion | flops 8912896 | bytes 2097152 | tf_op jit(solution)/shard_map/convert.10
  24.3 0.2 copy.43
  24.5 2.9 %convolution_bitcast_fusion = f32[16,8,2048]{2,1,0:T(8,128)S(1)} fusion(bf16[128,1024]{1,0:T(8,128)(2,1)S(1)} %reshape.22, bf16[1024,2048]{1,0:T(8,128)(2,1)} %shard_map.37), kind=kOutput, calls=%fused_computation.17 | convolution fusion | flops 536870912 | bytes 5505024 | tf_op jit(solution)/shard_map/dot_general | solution.py:62
  27.5 0.5 fusion.9
  28.0 0.7 fusion.18
  28.8 2.1 copy.44
  30.9 2.2 reshape.54
  33.1 9.6 %all_to_all.34 = bf16[4,2,16384]{2,1,0:T(2,128)(2,1)S(1)} all-to-all(bf16[4,2,16384]{2,1,0:T(2,128)(2,1)S(1)} %reshape.54), channel_id=1, replica_groups=mesh['zy'=32,'c'=2,'tm'=4] {'tm'}, dimensions={0} | all-to-all | bytes 524288 | tf_op jit(solution)/shard_map/all_to_all | solution.py:84
  42.7 1.4 reshape.55
  44.1 1.9 copy.80
  46.0 0.7 copy.46
  46.8 0.2 all-gather.6.cloned.1.call-start
  47.0 100.2 %all-gather.4.cloned.1.call-done = bf16[32,64,8,2,128]{4,2,3,1,0:T(8,128)(2,1)} async-done(((bf16[1,64,8,2,128]{4,2,3,1,0:T(8,128)(2,1)}), bf16[32,64,8,2,128]{4,2,3,1,0:T(8,128)(2,1)}) %all-gather.4.cloned.1.call-update) | async-done | bytes 8388624 | tf_op jit(solution)/shard_map/all_gather | solution.py:86
  147.2 0.7 copy-done.1
  148.2 34.7 %all-gather.6.cloned.1.call-done = bf16[64,64,8,2,128]{4,2,3,1,0:T(8,128)(2,1)} async-done(((bf16[32,64,8,2,128]{4,2,3,1,0:T(8,128)(2,1)}), bf16[64,64,8,2,128]{4,2,3,1,0:T(8,128)(2,1)}) %all-gather.6.cloned.1.call-update) | async-done | bytes 16777232 | tf_op jit(solution)/shard_map/all_gather | solution.py:87
  183.0 18.8 %gather_fusion = bf16[128,64,8,2,128]{4,2,3,1,0:T(8,128)(2,1)} fusion(bf16[2,32,64,8,2,128]{5,3,4,2,1,0:T(8,128)(2,1)} %bitcast.72, s32[128]{0:T(128)S(1)} %reshape.27), kind=kCustom, calls=%fused_computation | custom fusion | bytes 67109888 | tf_op jit(solution)/shard_map/gather | solution.py:88
  201.8 50.4 %fusion.2 = (f32[64,128,2,64]{1,3,2,0:T(8,128)}, f32[64,128,2,64]{1,3,2,0:T(8,128)S(1)}, f32[64,128,2,64]{1,3,2,0:T(8,128)S(1)}, f32[64,128,2,64]{1,3,2,0:T(8,128)}) fusion(f32[64,128,8]{1,2,0:T(8,128)S(1)} %get-tuple-element.12, bf16[64,2,64,8,2,128]{5,3,4,2,1,0:T(8,128)(2,1)} %bitcast.71, f32[64,128,8]{1,2,0:T(8,128)S(1)} %get-tuple-element.11), kind=kLoop, calls=%fused_computation.7 | loop fusion | flops 79691776 | bytes 50855936 | tf_op jit(solution)/shard_map/swf,skjwf->skjf/dot_general | solution.py:91
  252.2 4.5 %fusion.7 = bf16[64,2,64,1,128]{4,2,1,0,3:T(8,128)(2,1)S(1)} fusion(f32[64,128,2,64]{1,3,2,0:T(8,128)} %get-tuple-element.10, f32[64,128,2,64]{1,3,2,0:T(8,128)} %get-tuple-element.5), kind=kLoop, calls=%fused_computation.21 | loop fusion | flops 2097152 | bytes 10485760 | tf_op jit(solution)/shard_map/stack | solution.py:101
  256.7 1.0 fusion.8
  257.7 0.4 pad_maximum_fusion
  258.1 10.5 %copy.51 = bf16[64,2,64,2,128]{4,3,2,1,0:T(2,128)(2,1)} copy(bf16[64,2,64,2,128]{4,2,1,0,3:T(8,128)(2,1)S(1)} %pad_maximum_fusion) | data formatting | bytes 8388608 | tf_op jit(solution)/shard_map/stack | solution.py:101
  (14 shorter events, 0.5 us)
Async XLA Ops:
  6.5 17.7 %all-to-all-start = ((bf16[4,16,2048]{2,1,0:T(8,128)(2,1)}), bf16[4,16,2048]{2,1,0:T(8,128)(2,1)S(1)}, u32[]{:S(2)}, u32[]{:S(2)}) async-start(bf16[4,16,2048]{2,1,0:T(8,128)(2,1)} %bitcast.80), calls=%async_computation | async-start | bytes 524288 | tf_op jit(solution)/shard_map/all_to_all | solution.py:58
  11.4 135.8 %all-gather.4.cloned.1.call-start = ((), (), s32[]{:S(2)}) async-start(), calls=%async_computation.2 | async-start | bytes 8650752 | tf_op jit(solution)/shard_map/all_gather | solution.py:86
  46.8 136.2 %all-gather.6.cloned.1.call-start = ((), (), s32[]{:S(2)}) async-start(), calls=%async_computation.3 | async-start | bytes 25165824 | tf_op jit(solution)/shard_map/all_gather | solution.py:87
  147.2 0.7 copy-start.1
  147.2 1.0 copy-start
Sparse Core Ops, SparseCore 0:
  46.9 100.2 all-gather.3
  149.0 33.9 all-gather.5
where the time goes:
time: 276 us; the launch traced here: 275 us
  waiting for transfers between devices  135 us (49%)
  other arithmetic  66.2 us (24%)
  local copies, waits for them, and re-layouts  38.9 us (14%)
  between operations  13.5 us (5%)
  blocking collectives  9.57 us (3%)
  starting transfers between devices  5.05 us (2%)
  matrix products  4.1 us (1%)
  Pallas kernels  3.05 us (1%)
    all_gather x1, waiting for transfers between devices, shards(): same_core = lax.all_gather(regrouped, 'zy', axis=0, tiled=False)  100 us
    dot_general x1, other arithmetic, block_sum(): jnp.einsum('swf,skjwf->skjf', left_part, right_part, preferred_element_ty...  50.4 us
    all_gather x1, waiting for transfers between devices, shards(): both_cores = lax.all_gather(same_core, 'c', axis=0, tiled=False)  34.7 us
    gather x1, local copies, waits for them, and re-layouts, shards(): needed = both_cores[station_owners % CORES, station_owners // CORES]  18.8 us
    another operation x1, local copies, waits for them, and re-layouts, shards(): result = jnp.stack([real_sum, imag_sum], axis=3).astype(jnp.bfloat16)  10.5 us
    all_to_all x1, blocking collectives, shards(): lax.all_to_all(whitened, 'tm', split_axis=3, concat_axis=0, tiled=True)  9.57 us
    another operation x1, other arithmetic  8.54 us
    another operation x3, other arithmetic, shards(): result = jnp.stack([real_sum, imag_sum], axis=3).astype(jnp.bfloat16)  5.92 us
  transfers between devices with their start and end apart: 3, of which 2 were waited for; matrix products, arithmetic and copies ran while one was open for 4% of the time, Pallas kernels for 1%

commit v1 on v0

--- a/solution.py
+++ b/solution.py
@@ -5,7 +5,6 @@
 from jax import lax
 from jax.experimental import pallas as pl
 from jax.experimental.pallas import tpu as pltpu
-from jax.sharding import Mesh
 from jax.sharding import PartitionSpec as P
 
 WIN = 1024
@@ -54,6 +53,66 @@
     return inside.astype(jnp.float32)
 
 
+ROWS = 32
+
+
+def corr_kernel(owner_ref, part_ref, own_ref, out_hbm, scr, sem):
+    rows_all, freq = part_ref.shape[2], part_ref.shape[3]
+    n_pairs = owner_ref.shape[0]
+    n_top = out_hbm.shape[1]
+    chunk = min(ROWS, rows_all)
+    row_id = lax.broadcasted_iota(jnp.int32, (chunk, freq), 0)
+    even = (row_id % 2) == 0
+    sign = jnp.where(even, 1.0, -1.0).astype(jnp.float32)
+
+    def one(i, carry):
+        slot = i % 2
+        s = i // n_top
+        k = i % n_top
+        b = owner_ref[i]
+
+        @pl.when(i >= 2)
+        def _():
+            pltpu.make_async_copy(scr.at[slot], out_hbm.at[0, 0], sem.at[slot]).wait()
+
+        for c0 in range(0, rows_all, chunk):
+            acc1 = jnp.zeros((chunk, freq), jnp.float32)
+            acc2 = jnp.zeros((chunk, freq), jnp.float32)
+            for w in range(NW):
+                q = part_ref[b, w, c0 : c0 + chunk, :].astype(jnp.float32)
+                sre = own_ref[s, 2 * w : 2 * w + 1, :].astype(jnp.float32)
+                sim = own_ref[s, 2 * w + 1 : 2 * w + 2, :].astype(jnp.float32)
+                acc1 = acc1 + q * sre
+                acc2 = acc2 + q * sim
+            up = pltpu.roll(acc2, chunk - 1, 0)
+            dn = pltpu.roll(acc2, 1, 0)
+            res = sign * acc1 + jnp.where(even, up, dn)
+            scr[slot, c0 : c0 + chunk, :] = res.astype(scr.dtype)
+        pltpu.make_async_copy(scr.at[slot], out_hbm.at[s, k], sem.at[slot]).start()
+        return carry
+
+    lax.fori_loop(0, n_pairs, one, 0)
+    for back in range(min(2, n_pairs)):
+        last = n_pairs - 1 - back
+        pltpu.make_async_copy(scr.at[last % 2], out_hbm.at[0, 0], sem.at[last % 2]).wait()
+
+
+def correlate(owners, part, own, out_shape):
+    rows, freq = part.shape[2], part.shape[3]
+    return pl.pallas_call(
+        corr_kernel,
+        out_shape=jax.ShapeDtypeStruct(out_shape, jnp.bfloat16),
+        in_specs=[
+            pl.BlockSpec(memory_space=pltpu.SMEM),
+            pl.BlockSpec(memory_space=pltpu.VMEM),
+            pl.BlockSpec(memory_space=pltpu.VMEM),
+        ],
+        out_specs=pl.BlockSpec(memory_space=pl.ANY),
+        scratch_shapes=[pltpu.VMEM((2, rows, freq), jnp.bfloat16), pltpu.SemaphoreType.DMA((2,))],
+        compiler_params=pltpu.CompilerParams(vmem_limit_bytes=48 * 1024 * 1024),
+    )(owners, part, own)
+
+
 def shards(records, band_taps, station_owners):
     relayed = lax.all_to_all(records, "tm", split_axis=0, concat_axis=1, tiled=True)
     station_count = relayed.shape[0]
@@ -83,36 +142,21 @@
     whitened = whitened.reshape(station_count, NW, 2, FREQ)
     regrouped = lax.all_to_all(whitened, "tm", split_axis=3, concat_axis=0, tiled=True)
     own_count = regrouped.shape[0]
-    same_core = lax.all_gather(regrouped, "zy", axis=0, tiled=False)
-    both_cores = lax.all_gather(same_core, "c", axis=0, tiled=False)
-    needed = both_cores[station_owners % CORES, station_owners // CORES]
-
-    def block_sum(left_part, right_part):
-        return jnp.einsum(
-            "swf,skjwf->skjf", left_part, right_part, preferred_element_type=jnp.float32
-        )
-
-    sig_re = regrouped[:, :, 0]
-    sig_im = regrouped[:, :, 1]
-    par_re = needed[..., 0, :]
-    par_im = needed[..., 1, :]
-    real_sum = block_sum(sig_re, par_re) + block_sum(sig_im, par_im)
-    imag_sum = block_sum(sig_im, par_re) - block_sum(sig_re, par_im)
-    result = jnp.stack([real_sum, imag_sum], axis=3).astype(jnp.bfloat16)
-    return result
+    freq = regrouped.shape[3]
+    contribution = regrouped.transpose(1, 0, 2, 3).reshape(NW, own_count * 2, freq)
+    gathered = lax.all_gather(contribution, "sta", axis=0, tiled=False)
+    own = regrouped.reshape(own_count, NW * 2, freq)
+    out_shape = (own_count, station_owners.shape[1], own_count * 2, freq)
+    result = correlate(station_owners.reshape(-1), gathered, own, out_shape)
+    return result.reshape(own_count, station_owners.shape[1], own_count, 2, freq)
 
 
 def solution(mesh):
-    n_sta, n_tm = mesh.shape["sta"], mesh.shape["tm"]
-    split_mesh = Mesh(
-        mesh.devices.reshape(n_sta // CORES, CORES, n_tm), ("zy", "c", "tm")
-    )
-    sta = ("zy", "c")
-    placed = (P(sta, "tm"), P(), P(sta, None))
+    placed = (P("sta", "tm"), P(), P("sta", None))
     return jax.shard_map(
         shards,
-        mesh=split_mesh,
+        mesh=mesh,
         in_specs=placed,
-        out_specs=P(sta, None, None, None, "tm"),
+        out_specs=P("sta", None, None, None, "tm"),
         check_vma=False,
     )

time: 276 us -> 209 us (0.76)
  other arithmetic: 66.2 us -> 9.9 us
  Pallas kernels: 3.05 us -> 55.2 us
  waiting for transfers between devices: 135 us -> 103 us
  local copies, waits for them, and re-layouts: 38.9 us -> 9.15 us
    pallas_call x0 -> x1, Pallas kernels: none -> 52.2 us  [correlate(): pl.pallas_call(corr_kernel, out_shape=jax.ShapeDtypeStruct(out_shape, jnp...]
    dot_general x1 -> x0, other arithmetic: 50.4 us -> none  [block_sum(): jnp.einsum('swf,skjwf->skjf', left_part, right_part, preferred_element_ty...]
    all_gather x2 -> x1, waiting for transfers between devices: 135 us -> 102 us  [shards(): gathered = lax.all_gather(contribution, 'sta', axis=0, tiled=False)]
    gather x1 -> x0, local copies, waits for them, and re-layouts: 18.8 us -> none  [shards(): needed = both_cores[station_owners % CORES, station_owners // CORES]]
    another operation x1, local copies, waits for them, and re-layouts: 10.5 us -> 0.75 us  [shards(): gathered = lax.all_gather(contribution, 'sta', axis=0, tiled=False)]
    another operation x4 -> x1, other arithmetic: 14.5 us -> 8.54 us
  transfers between devices with their start and end apart: 3 -> 2, of which waited for: 2 -> 1; matrix products, arithmetic and copies ran while one was open for 4% -> 5% of each run, Pallas kernels for 1% -> 1%
where the time goes in v1:
time: 209 us
  waiting for transfers between devices  103 us (49%)
  Pallas kernels  55.2 us (26%)
  between operations  13.5 us (6%)
  other arithmetic  9.9 us (5%)
  blocking collectives  9.57 us (5%)
  local copies, waits for them, and re-layouts  9.15 us (4%)
  starting transfers between devices  4.83 us (2%)
  matrix products  4.1 us (2%)
    all_gather x1, waiting for transfers between devices, shards(): gathered = lax.all_gather(contribution, 'sta', axis=0, tiled=False)  102 us
    pallas_call x1, Pallas kernels, correlate(): pl.pallas_call(corr_kernel, out_shape=jax.ShapeDtypeStruct(out_shape, jnp...  52.2 us
    all_to_all x1, blocking collectives, shards(): lax.all_to_all(whitened, 'tm', split_axis=3, concat_axis=0, tiled=True)  9.57 us
    another operation x1, other arithmetic  8.54 us
    all_to_all x1, starting transfers between devices, shards(): lax.all_to_all(records, 'tm', split_axis=0, concat_axis=1, tiled=True)  4.83 us
  transfers between devices with their start and end apart: 2, of which 1 were waited for; matrix products, arithmetic and copies ran while one was open for 5% of the time, Pallas kernels for 1%

profile of v1, /device:TPU:1, one launch (start us, length us, event | category | flops | bytes accessed | tf_op | source)
XLA Modules:
  0.0 208.8 jit_solution(5043646735263440381)
XLA Ops:
  6.5 4.8 %all-to-all-start = ((bf16[4,16,2048]{2,1,0:T(8,128)(2,1)}), bf16[4,16,2048]{2,1,0:T(8,128)(2,1)S(1)}, u32[]{:S(2)}, u32[]{:S(2)}) async-start(bf16[4,16,2048]{2,1,0:T(8,128)(2,1)} %bitcast.34), calls=%async_computation | async-start | bytes 524288 | tf_op jit(solution)/shard_map/all_to_all | solution.py:117
  11.4 1.3 pad_convert_fusion
  12.7 3.1 %shard_map.37 = bf16[1024,2048]{1,0:T(8,128)(2,1)} custom-call(f32[1,2048]{1,0:T(1,128)} %bitcast.35), custom_call_target="tpu_custom_call" | custom-call | tf_op jit(solution)/shard_map/pallas_call | solution.py:30
  15.7 8.5 %negate_convert_fusion = (bf16[1024,512]{1,0:T(8,128)(2,1)S(1)}, bf16[1024,512]{1,0:T(8,128)(2,1)S(1)}) fusion(), kind=kLoop, calls=%fused_computation.11 | loop fusion | flops 8912896 | bytes 2097152 | tf_op jit(solution)/shard_map/convert.4
  24.3 0.0 all-to-all-done
  24.3 0.2 copy.31
  24.5 0.1 reshape.32
  24.5 2.9 %convolution_bitcast_fusion = f32[16,8,2048]{2,1,0:T(8,128)S(1)} fusion(bf16[128,1024]{1,0:T(8,128)(2,1)S(1)} %reshape.32, bf16[1024,2048]{1,0:T(8,128)(2,1)} %shard_map.37), kind=kOutput, calls=%fused_computation.3 | convolution fusion | flops 536870912 | bytes 5505024 | tf_op jit(solution)/shard_map/dot_general | solution.py:121
  27.5 0.5 fusion.3
  28.0 0.7 fusion.12
  28.7 0.1 multiply_convert_fusion
  28.8 2.1 copy.32
  30.9 2.2 %reshape.39 = bf16[4,2,16384]{2,1,0:T(2,128)(2,1)S(1)} reshape(bf16[512,2,8,16]{3,2,1,0:T(8,128)(2,1)S(1)} %bitcast.27) | data formatting | bytes 524288
  33.1 9.6 %all_to_all.34 = bf16[4,2,16384]{2,1,0:T(2,128)(2,1)S(1)} all-to-all(bf16[4,2,16384]{2,1,0:T(2,128)(2,1)S(1)} %reshape.39), channel_id=1, replica_groups=mesh['sta'=64,'tm'=4] {'tm'}, dimensions={0} | all-to-all | bytes 524288 | tf_op jit(solution)/shard_map/all_to_all | solution.py:143
  42.7 1.4 reshape.40
  44.1 0.0 copy-start
  44.1 1.9 copy.37
  46.1 0.7 copy.35
  46.8 0.0 all-gather.2.cloned.1.call-update
  46.9 0.1 copy.30
  47.0 0.1 reshape.31.owner_ref
  47.1 0.2 copy.36
  47.3 102.5 %all-gather.2.cloned.1.call-done.part_ref = bf16[64,8,128,128]{3,2,1,0:T(8,128)(2,1)} async-done(((bf16[1,8,128,128]{3,2,1,0:T(8,128)(2,1)}), bf16[64,8,128,128]{3,2,1,0:T(8,128)(2,1)}) %all-gather.2.cloned.1.call-update) | async-done | bytes 16777232 | tf_op jit(solution)/shard_map/all_gather | solution.py:147
  149.8 52.2 %shard_map.38 = bf16[64,2,128,128]{3,2,1,0:T(8,128)(2,1)} custom-call(s32[128]{0:T(128)S(1)} %reshape.31.owner_ref, bf16[64,8,128,128]{3,2,1,0:T(8,128)(2,1)} %all-gather.2.cloned.1.call-done.part_ref, bf16[64,16,128]{2,1,0:T(8,128)(2,1)S(1)} %bitcast.26), custom_call_target="tpu_custom_call" | custom-call | tf_op jit(solution)/shard_map/pallas_call | solution.py:102
  (4 shorter events, 0.1 us)
Async XLA Ops:
  6.5 17.7 %all-to-all-start = ((bf16[4,16,2048]{2,1,0:T(8,128)(2,1)}), bf16[4,16,2048]{2,1,0:T(8,128)(2,1)S(1)}, u32[]{:S(2)}, u32[]{:S(2)}) async-start(bf16[4,16,2048]{2,1,0:T(8,128)(2,1)} %bitcast.34), calls=%async_computation | async-start | bytes 524288 | tf_op jit(solution)/shard_map/all_to_all | solution.py:117
  11.4 138.4 %all-gather.2.cloned.1.call-start = ((), (), s32[]{:S(2)}) async-start(), calls=%async_computation.2 | async-start | bytes 17039360 | tf_op jit(solution)/shard_map/all_gather | solution.py:147
  44.1 2.8 %copy-start = (s32[64,2]{0,1:T(2,128)S(1)}, s32[64,2]{0,1:T(2,128)}, u32[]{:S(2)}) copy-start(s32[64,2]{0,1:T(2,128)} %param.5) | copy-start | bytes 1540
Sparse Core Ops, SparseCore 0:
  47.0 102.7 all-gather.1

commit v2 on v1

--- a/solution.py
+++ b/solution.py
@@ -1,3 +1,4 @@
+import functools
 import math
 
 import jax
@@ -53,15 +54,15 @@
     return inside.astype(jnp.float32)
 
 
-ROWS = 32
+SUB = 8
 
 
-def corr_kernel(owner_ref, part_ref, own_ref, out_hbm, scr, sem):
-    rows_all, freq = part_ref.shape[2], part_ref.shape[3]
+def corr_kernel(owner_ref, part_ref, own_ref, *rest, row0):
+    out_hbm, scr, sem = rest[-3], rest[-2], rest[-1]
+    n_blocks, n_win, rows, freq = part_ref.shape
     n_pairs = owner_ref.shape[0]
     n_top = out_hbm.shape[1]
-    chunk = min(ROWS, rows_all)
-    row_id = lax.broadcasted_iota(jnp.int32, (chunk, freq), 0)
+    row_id = lax.broadcasted_iota(jnp.int32, (rows, freq), 0)
     even = (row_id % 2) == 0
     sign = jnp.where(even, 1.0, -1.0).astype(jnp.float32)
 
@@ -73,44 +74,61 @@
 
         @pl.when(i >= 2)
         def _():
-            pltpu.make_async_copy(scr.at[slot], out_hbm.at[0, 0], sem.at[slot]).wait()
+            pltpu.make_async_copy(
+                scr.at[slot], out_hbm.at[0, 0, pl.ds(row0, rows)], sem.at[slot]
+            ).wait()
 
-        for c0 in range(0, rows_all, chunk):
-            acc1 = jnp.zeros((chunk, freq), jnp.float32)
-            acc2 = jnp.zeros((chunk, freq), jnp.float32)
-            for w in range(NW):
-                q = part_ref[b, w, c0 : c0 + chunk, :].astype(jnp.float32)
-                sre = own_ref[s, 2 * w : 2 * w + 1, :].astype(jnp.float32)
-                sim = own_ref[s, 2 * w + 1 : 2 * w + 2, :].astype(jnp.float32)
-                acc1 = acc1 + q * sre
-                acc2 = acc2 + q * sim
-            up = pltpu.roll(acc2, chunk - 1, 0)
-            dn = pltpu.roll(acc2, 1, 0)
-            res = sign * acc1 + jnp.where(even, up, dn)
-            scr[slot, c0 : c0 + chunk, :] = res.astype(scr.dtype)
-        pltpu.make_async_copy(scr.at[slot], out_hbm.at[s, k], sem.at[slot]).start()
+        acc1 = jnp.zeros((rows // SUB, SUB, freq), jnp.float32)
+        acc2 = jnp.zeros((rows // SUB, SUB, freq), jnp.float32)
+        for w in range(n_win):
+            q = part_ref[b, w].astype(jnp.float32).reshape(rows // SUB, SUB, freq)
+            sre = jnp.broadcast_to(own_ref[s, 2 * w : 2 * w + 1, :], (SUB, freq))
+            sim = jnp.broadcast_to(own_ref[s, 2 * w + 1 : 2 * w + 2, :], (SUB, freq))
+            acc1 = acc1 + q * sre[None]
+            acc2 = acc2 + q * sim[None]
+        acc1 = acc1.reshape(rows, freq)
+        acc2 = acc2.reshape(rows, freq)
+        up = pltpu.roll(acc2, rows - 1, 0)
+        dn = pltpu.roll(acc2, 1, 0)
+        scr[slot] = (sign * acc1 + jnp.where(even, up, dn)).astype(scr.dtype)
+        pltpu.make_async_copy(
+            scr.at[slot], out_hbm.at[s, k, pl.ds(row0, rows)], sem.at[slot]
+        ).start()
         return carry
 
     lax.fori_loop(0, n_pairs, one, 0)
     for back in range(min(2, n_pairs)):
         last = n_pairs - 1 - back
-        pltpu.make_async_copy(scr.at[last % 2], out_hbm.at[0, 0], sem.at[last % 2]).wait()
+        pltpu.make_async_copy(
+            scr.at[last % 2], out_hbm.at[0, 0, pl.ds(row0, rows)], sem.at[last % 2]
+        ).wait()
 
 
-def correlate(owners, part, own, out_shape):
+def correlate(owners, part, own, out_shape, row0, prior=None):
     rows, freq = part.shape[2], part.shape[3]
+    in_specs = [
+        pl.BlockSpec(memory_space=pltpu.SMEM),
+        pl.BlockSpec(memory_space=pltpu.VMEM),
+        pl.BlockSpec(memory_space=pltpu.VMEM),
+    ]
+    args = [owners, part, own]
+    aliases = {}
+    if prior is not None:
+        in_specs.append(pl.BlockSpec(memory_space=pl.ANY))
+        args.append(prior)
+        aliases = {len(args) - 1: 0}
     return pl.pallas_call(
-        corr_kernel,
+        functools.partial(corr_kernel, row0=row0),
         out_shape=jax.ShapeDtypeStruct(out_shape, jnp.bfloat16),
-        in_specs=[
-            pl.BlockSpec(memory_space=pltpu.SMEM),
-            pl.BlockSpec(memory_space=pltpu.VMEM),
-            pl.BlockSpec(memory_space=pltpu.VMEM),
+        in_specs=in_specs,
+        out_specs=pl.BlockSpec(memory_space=pl.ANY),
+        scratch_shapes=[
+            pltpu.VMEM((2, rows, freq), jnp.bfloat16),
+            pltpu.SemaphoreType.DMA((2,)),
         ],
-        out_specs=pl.BlockSpec(memory_space=pl.ANY),
-        scratch_shapes=[pltpu.VMEM((2, rows, freq), jnp.bfloat16), pltpu.SemaphoreType.DMA((2,))],
-        compiler_params=pltpu.CompilerParams(vmem_limit_bytes=48 * 1024 * 1024),
-    )(owners, part, own)
+        input_output_aliases=aliases,
+        compiler_params=pltpu.CompilerParams(vmem_limit_bytes=40 * 1024 * 1024),
+    )(*args)
 
 
 def shards(records, band_taps, station_owners):
@@ -144,10 +162,14 @@
     own_count = regrouped.shape[0]
     freq = regrouped.shape[3]
     contribution = regrouped.transpose(1, 0, 2, 3).reshape(NW, own_count * 2, freq)
-    gathered = lax.all_gather(contribution, "sta", axis=0, tiled=False)
-    own = regrouped.reshape(own_count, NW * 2, freq)
+    half = own_count
+    own = regrouped.astype(jnp.float32).reshape(own_count, NW * 2, freq)
     out_shape = (own_count, station_owners.shape[1], own_count * 2, freq)
-    result = correlate(station_owners.reshape(-1), gathered, own, out_shape)
+    owners = station_owners.reshape(-1)
+    first_rows = lax.all_gather(contribution[:, :half], "sta", axis=0, tiled=False)
+    second_rows = lax.all_gather(contribution[:, half:], "sta", axis=0, tiled=False)
+    result = correlate(owners, first_rows, own, out_shape, 0)
+    result = correlate(owners, second_rows, own, out_shape, half, prior=result)
     return result.reshape(own_count, station_owners.shape[1], own_count, 2, freq)
 
 

time: 209 us -> 269 us (1.29)
  Pallas kernels: 55.2 us -> 89 us
  waiting for transfers between devices: 103 us -> 122 us
  local copies, waits for them, and re-layouts: 9.15 us -> 16.5 us
    pallas_call x1 -> x2, Pallas kernels: 52.2 us -> 86 us  [correlate(): pl.pallas_call(functools.partial(corr_kernel, row0=row0), out_shape=jax.S...]
    all_gather x1 -> x2, waiting for transfers between devices: 102 us -> 122 us  [the longest x1 85.3 us: shards(): lax.all_gather(contribution[:, :half], 'sta', axis=0, tiled=False)]
    unnamed x5 -> x11, local copies, waits for them, and re-layouts: 3.72 us -> 11.8 us
  transfers between devices with their start and end apart: 2 -> 3, of which waited for: 1 -> 2; matrix products, arithmetic and copies ran while one was open for 5% -> 4% of each run, Pallas kernels for 1% -> 17%
where the time goes in v2:
time: 269 us
  waiting for transfers between devices  122 us (45%)
  Pallas kernels  89 us (33%)
  local copies, waits for them, and re-layouts  16.5 us (6%)
  between operations  13.6 us (5%)
  other arithmetic  9.93 us (4%)
  blocking collectives  9.57 us (4%)
  starting transfers between devices  4.87 us (2%)
  matrix products  4.1 us (2%)
    pallas_call x2, Pallas kernels, correlate(): pl.pallas_call(functools.partial(corr_kernel, row0=row0), out_shape=jax.S...  86 us
    all_gather x1, waiting for transfers between devices, shards(): lax.all_gather(contribution[:, :half], 'sta', axis=0, tiled=False)  85.3 us
    all_gather x1, waiting for transfers between devices, shards(): lax.all_gather(contribution[:, half:], 'sta', axis=0, tiled=False)  36.2 us
    unnamed x11, local copies, waits for them, and re-layouts  11.8 us
    all_to_all x1, blocking collectives, shards(): lax.all_to_all(whitened, 'tm', split_axis=3, concat_axis=0, tiled=True)  9.57 us
    another operation x1, other arithmetic  8.54 us
  transfers between devices with their start and end apart: 3, of which 2 were waited for; matrix products, arithmetic and copies ran while one was open for 4% of the time, Pallas kernels for 17%

profile of v2, /device:TPU:1, one launch (start us, length us, event | category | flops | bytes accessed | tf_op | source)
XLA Modules:
  0.0 269.1 jit_solution(6636497336840739544)
XLA Ops:
  6.5 4.8 %all-to-all-start = ((bf16[4,16,2048]{2,1,0:T(8,128)(2,1)}), bf16[4,16,2048]{2,1,0:T(8,128)(2,1)S(1)}, u32[]{:S(2)}, u32[]{:S(2)}) async-start(bf16[4,16,2048]{2,1,0:T(8,128)(2,1)} %bitcast.39), calls=%async_computation | async-start | bytes 524288 | tf_op jit(solution)/shard_map/all_to_all | solution.py:135
  11.4 1.3 pad_convert_fusion
  12.6 3.1 %shard_map.37 = bf16[1024,2048]{1,0:T(8,128)(2,1)} custom-call(f32[1,2048]{1,0:T(1,128)} %bitcast.40), custom_call_target="tpu_custom_call" | custom-call | tf_op jit(solution)/shard_map/pallas_call | solution.py:31
  15.7 8.5 %negate_convert_fusion = (bf16[1024,512]{1,0:T(8,128)(2,1)S(1)}, bf16[1024,512]{1,0:T(8,128)(2,1)S(1)}) fusion(), kind=kLoop, calls=%fused_computation.11 | loop fusion | flops 8912896 | bytes 2097152 | tf_op jit(solution)/shard_map/convert.5
  24.3 0.2 copy.35
  24.5 2.9 %convolution_bitcast_fusion = f32[16,8,2048]{2,1,0:T(8,128)S(1)} fusion(bf16[128,1024]{1,0:T(8,128)(2,1)S(1)} %reshape.35, bf16[1024,2048]{1,0:T(8,128)(2,1)} %shard_map.37), kind=kOutput, calls=%fused_computation.3 | convolution fusion | flops 536870912 | bytes 5505024 | tf_op jit(solution)/shard_map/dot_general | solution.py:139
  27.5 0.5 fusion.3
  28.0 0.7 fusion.12
  28.8 2.1 copy.36
  30.9 2.2 reshape.45
  33.1 9.6 %all_to_all.34 = bf16[4,2,16384]{2,1,0:T(2,128)(2,1)S(1)} all-to-all(bf16[4,2,16384]{2,1,0:T(2,128)(2,1)S(1)} %reshape.45), channel_id=1, replica_groups=mesh['sta'=64,'tm'=4] {'tm'}, dimensions={0} | all-to-all | bytes 524288 | tf_op jit(solution)/shard_map/all_to_all | solution.py:161
  42.7 1.4 reshape.46
  44.1 1.8 copy.38
  45.9 0.7 copy.45
  46.7 0.7 copy.44
  47.4 0.1 copy.34
  47.5 0.1 reshape.34.owner_ref
  47.7 0.3 copy.40
  48.0 85.3 %all-gather.7.cloned.1.call-done = bf16[512,64,128]{2,1,0:T(8,128)(2,1)} async-done(((bf16[8,64,128]{2,1,0:T(8,128)(2,1)}), bf16[512,64,128]{2,1,0:T(8,128)(2,1)}) %all-gather.7.cloned.1.call-update) | async-done | bytes 8388624 | tf_op jit(solution)/shard_map/all_gather | solution.py:169
  133.3 3.4 %copy-done = bf16[512,64,128]{2,1,0:T(8,128)(2,1)S(1)} copy-done((bf16[512,64,128]{2,1,0:T(8,128)(2,1)S(1)}, bf16[512,64,128]{2,1,0:T(8,128)(2,1)}, u32[]{:S(2)}) %copy-start) | copy-done | bytes 8388632
  136.7 43.0 %shard_map.38.rest_0_ = bf16[64,2,128,128]{3,2,1,0:T(8,128)(2,1)} custom-call(s32[128]{0:T(128)S(1)} %reshape.34.owner_ref, bf16[64,8,64,128]{3,2,1,0:T(8,128)(2,1)S(1)} %bitcast.30, f32[64,16,128]{2,1,0:T(8,128)S(1)} %bitcast.32), custom_call_target="tpu_custom_call" | custom-call | tf_op jit(solution)/shard_map/pallas_call | solution.py:120
  179.7 36.2 %all-gather.5.cloned.1.call-done = bf16[512,64,128]{2,1,0:T(8,128)(2,1)} async-done(((bf16[8,64,128]{2,1,0:T(8,128)(2,1)}), bf16[512,64,128]{2,1,0:T(8,128)(2,1)}) %all-gather.5.cloned.1.call-update) | async-done | bytes 8388624 | tf_op jit(solution)/shard_map/all_gather | solution.py:170
  215.9 3.4 %copy-done.1 = bf16[512,64,128]{2,1,0:T(8,128)(2,1)S(1)} copy-done((bf16[512,64,128]{2,1,0:T(8,128)(2,1)S(1)}, bf16[512,64,128]{2,1,0:T(8,128)(2,1)}, u32[]{:S(2)}) %copy-start.1) | copy-done | bytes 8388632
  219.3 43.0 %shard_map.39 = bf16[64,2,128,128]{3,2,1,0:T(8,128)(2,1)} custom-call(s32[128]{0:T(128)S(1)} %reshape.34.owner_ref, bf16[64,8,64,128]{3,2,1,0:T(8,128)(2,1)S(1)} %bitcast.31, f32[64,16,128]{2,1,0:T(8,128)S(1)} %bitcast.33, bf16[64,2,128,128]{3,2,1,0:T(8,128)(2,1)} %shard_map.38.rest_0_), custom_call_target="tpu_custom_call", output_to_operand_aliasing={{}: (3, {})} | custom-call | tf_op jit(solution)/shard_map/pallas_call | solution.py:120
  (14 shorter events, 0.3 us)
Async XLA Ops:
  6.5 17.7 %all-to-all-start = ((bf16[4,16,2048]{2,1,0:T(8,128)(2,1)}), bf16[4,16,2048]{2,1,0:T(8,128)(2,1)S(1)}, u32[]{:S(2)}, u32[]{:S(2)}) async-start(bf16[4,16,2048]{2,1,0:T(8,128)(2,1)} %bitcast.39), calls=%async_computation | async-start | bytes 524288 | tf_op jit(solution)/shard_map/all_to_all | solution.py:135
  11.4 121.9 %all-gather.7.cloned.1.call-start = ((), (), s32[]{:S(2)}) async-start(), calls=%async_computation.3 | async-start | bytes 8519680 | tf_op jit(solution)/shard_map/all_gather | solution.py:169
  44.1 3.3 %copy-start.2 = (s32[64,2]{0,1:T(2,128)S(1)}, s32[64,2]{0,1:T(2,128)}, u32[]{:S(2)}) copy-start(s32[64,2]{0,1:T(2,128)} %param.5) | copy-start | bytes 1540
  46.6 169.3 %all-gather.5.cloned.1.call-start = ((), (), s32[]{:S(2)}) async-start(), calls=%async_computation.2 | async-start | bytes 8519680 | tf_op jit(solution)/shard_map/all_gather | solution.py:170
  133.3 3.4 %copy-start = (bf16[512,64,128]{2,1,0:T(8,128)(2,1)S(1)}, bf16[512,64,128]{2,1,0:T(8,128)(2,1)}, u32[]{:S(2)}) copy-start(bf16[512,64,128]{2,1,0:T(8,128)(2,1)} %all-gather.7.cloned.1.call-done) | copy-start | bytes 25165828
  215.9 3.4 %copy-start.1 = (bf16[512,64,128]{2,1,0:T(8,128)(2,1)S(1)}, bf16[512,64,128]{2,1,0:T(8,128)(2,1)}, u32[]{:S(2)}) copy-start(bf16[512,64,128]{2,1,0:T(8,128)(2,1)} %all-gather.5.cloned.1.call-done) | copy-start | bytes 25165828
Sparse Core Ops, SparseCore 0:
  46.8 86.4 all-gather.6
  136.1 79.7 all-gather.4

commit v3 on v1

--- a/solution.py
+++ b/solution.py
@@ -53,15 +53,15 @@
     return inside.astype(jnp.float32)
 
 
-ROWS = 32
+PACK = 16
 
 
 def corr_kernel(owner_ref, part_ref, own_ref, out_hbm, scr, sem):
-    rows_all, freq = part_ref.shape[2], part_ref.shape[3]
+    rows, freq = part_ref.shape[2], part_ref.shape[3]
+    n_win = part_ref.shape[1]
     n_pairs = owner_ref.shape[0]
     n_top = out_hbm.shape[1]
-    chunk = min(ROWS, rows_all)
-    row_id = lax.broadcasted_iota(jnp.int32, (chunk, freq), 0)
+    row_id = lax.broadcasted_iota(jnp.int32, (rows, freq), 0)
     even = (row_id % 2) == 0
     sign = jnp.where(even, 1.0, -1.0).astype(jnp.float32)
 
@@ -75,19 +75,19 @@
         def _():
             pltpu.make_async_copy(scr.at[slot], out_hbm.at[0, 0], sem.at[slot]).wait()
 
-        for c0 in range(0, rows_all, chunk):
-            acc1 = jnp.zeros((chunk, freq), jnp.float32)
-            acc2 = jnp.zeros((chunk, freq), jnp.float32)
-            for w in range(NW):
-                q = part_ref[b, w, c0 : c0 + chunk, :].astype(jnp.float32)
-                sre = own_ref[s, 2 * w : 2 * w + 1, :].astype(jnp.float32)
-                sim = own_ref[s, 2 * w + 1 : 2 * w + 2, :].astype(jnp.float32)
-                acc1 = acc1 + q * sre
-                acc2 = acc2 + q * sim
-            up = pltpu.roll(acc2, chunk - 1, 0)
-            dn = pltpu.roll(acc2, 1, 0)
-            res = sign * acc1 + jnp.where(even, up, dn)
-            scr[slot, c0 : c0 + chunk, :] = res.astype(scr.dtype)
+        acc1 = jnp.zeros((rows // PACK, PACK, freq), jnp.bfloat16)
+        acc2 = jnp.zeros((rows // PACK, PACK, freq), jnp.bfloat16)
+        for w in range(n_win):
+            q = part_ref[b, w].reshape(rows // PACK, PACK, freq)
+            sre = jnp.broadcast_to(own_ref[s, 2 * w : 2 * w + 1, :], (PACK, freq))
+            sim = jnp.broadcast_to(own_ref[s, 2 * w + 1 : 2 * w + 2, :], (PACK, freq))
+            acc1 = acc1 + q * sre.astype(jnp.bfloat16)[None]
+            acc2 = acc2 + q * sim.astype(jnp.bfloat16)[None]
+        acc1 = acc1.reshape(rows, freq).astype(jnp.float32)
+        acc2 = acc2.reshape(rows, freq).astype(jnp.float32)
+        up = pltpu.roll(acc2, rows - 1, 0)
+        dn = pltpu.roll(acc2, 1, 0)
+        scr[slot] = (sign * acc1 + jnp.where(even, up, dn)).astype(scr.dtype)
         pltpu.make_async_copy(scr.at[slot], out_hbm.at[s, k], sem.at[slot]).start()
         return carry
 
@@ -145,7 +145,7 @@
     freq = regrouped.shape[3]
     contribution = regrouped.transpose(1, 0, 2, 3).reshape(NW, own_count * 2, freq)
     gathered = lax.all_gather(contribution, "sta", axis=0, tiled=False)
-    own = regrouped.reshape(own_count, NW * 2, freq)
+    own = regrouped.astype(jnp.float32).reshape(own_count, NW * 2, freq)
     out_shape = (own_count, station_owners.shape[1], own_count * 2, freq)
     result = correlate(station_owners.reshape(-1), gathered, own, out_shape)
     return result.reshape(own_count, station_owners.shape[1], own_count, 2, freq)

time: 209 us -> 208 us (level)
  no operation moved by 1% of the time
where the time goes in v3:
time: 208 us
  waiting for transfers between devices  102 us (49%)
  Pallas kernels  54.5 us (26%)
  between operations  13.5 us (6%)
  other arithmetic  9.94 us (5%)
  blocking collectives  9.57 us (5%)
  local copies, waits for them, and re-layouts  9.06 us (4%)
  starting transfers between devices  4.83 us (2%)
  matrix products  4.1 us (2%)
    all_gather x1, waiting for transfers between devices, shards(): gathered = lax.all_gather(contribution, 'sta', axis=0, tiled=False)  102 us
    pallas_call x1, Pallas kernels, correlate(): pl.pallas_call(corr_kernel, out_shape=jax.ShapeDtypeStruct(out_shape, jnp...  51.4 us
    all_to_all x1, blocking collectives, shards(): lax.all_to_all(whitened, 'tm', split_axis=3, concat_axis=0, tiled=True)  9.57 us
    another operation x1, other arithmetic  8.54 us
    all_to_all x1, starting transfers between devices, shards(): lax.all_to_all(records, 'tm', split_axis=0, concat_axis=1, tiled=True)  4.83 us
  transfers between devices with their start and end apart: 2, of which 1 were waited for; matrix products, arithmetic and copies ran while one was open for 5% of the time, Pallas kernels for 1%

profile of v3, /device:TPU:1, one launch (start us, length us, event | category | flops | bytes accessed | tf_op | source)
XLA Modules:
  0.0 207.9 jit_solution(8981983440836173419)
XLA Ops:
  6.5 4.8 %all-to-all-start = ((bf16[4,16,2048]{2,1,0:T(8,128)(2,1)}), bf16[4,16,2048]{2,1,0:T(8,128)(2,1)S(1)}, u32[]{:S(2)}, u32[]{:S(2)}) async-start(bf16[4,16,2048]{2,1,0:T(8,128)(2,1)} %bitcast.34), calls=%async_computation | async-start | bytes 524288 | tf_op jit(solution)/shard_map/all_to_all | solution.py:117
  11.4 1.3 pad_convert_fusion
  12.7 3.1 %shard_map.37 = bf16[1024,2048]{1,0:T(8,128)(2,1)} custom-call(f32[1,2048]{1,0:T(1,128)} %bitcast.35), custom_call_target="tpu_custom_call" | custom-call | tf_op jit(solution)/shard_map/pallas_call | solution.py:30
  15.7 8.5 %negate_convert_fusion = (bf16[1024,512]{1,0:T(8,128)(2,1)S(1)}, bf16[1024,512]{1,0:T(8,128)(2,1)S(1)}) fusion(), kind=kLoop, calls=%fused_computation.11 | loop fusion | flops 8912896 | bytes 2097152 | tf_op jit(solution)/shard_map/convert.5
  24.3 0.0 all-to-all-done
  24.3 0.2 copy.31
  24.5 0.1 reshape.32
  24.5 2.9 %convolution_bitcast_fusion = f32[16,8,2048]{2,1,0:T(8,128)S(1)} fusion(bf16[128,1024]{1,0:T(8,128)(2,1)S(1)} %reshape.32, bf16[1024,2048]{1,0:T(8,128)(2,1)} %shard_map.37), kind=kOutput, calls=%fused_computation.3 | convolution fusion | flops 536870912 | bytes 5505024 | tf_op jit(solution)/shard_map/dot_general | solution.py:121
  27.5 0.5 fusion.3
  28.0 0.7 fusion.12
  28.7 0.1 multiply_convert_fusion
  28.8 2.1 copy.32
  30.9 2.2 %reshape.39 = bf16[4,2,16384]{2,1,0:T(2,128)(2,1)S(1)} reshape(bf16[512,2,8,16]{3,2,1,0:T(8,128)(2,1)S(1)} %bitcast.29) | data formatting | bytes 524288
  33.1 9.6 %all_to_all.34 = bf16[4,2,16384]{2,1,0:T(2,128)(2,1)S(1)} all-to-all(bf16[4,2,16384]{2,1,0:T(2,128)(2,1)S(1)} %reshape.39), channel_id=1, replica_groups=mesh['sta'=64,'tm'=4] {'tm'}, dimensions={0} | all-to-all | bytes 524288 | tf_op jit(solution)/shard_map/all_to_all | solution.py:143
  42.7 1.4 reshape.40
  44.1 0.0 copy-start
  44.1 1.8 copy.34
  45.9 0.7 copy.35
  46.7 0.0 all-gather.2.cloned.1.call-update
  46.7 0.1 copy.30
  46.8 0.1 reshape.31.owner_ref
  47.0 0.3 copy.36
  47.2 102.4 %all-gather.2.cloned.1.call-done.part_ref = bf16[64,8,128,128]{3,2,1,0:T(8,128)(2,1)} async-done(((bf16[1,8,128,128]{3,2,1,0:T(8,128)(2,1)}), bf16[64,8,128,128]{3,2,1,0:T(8,128)(2,1)}) %all-gather.2.cloned.1.call-update) | async-done | bytes 16777232 | tf_op jit(solution)/shard_map/all_gather | solution.py:147
  149.6 51.4 %shard_map.38 = bf16[64,2,128,128]{3,2,1,0:T(8,128)(2,1)} custom-call(s32[128]{0:T(128)S(1)} %reshape.31.owner_ref, bf16[64,8,128,128]{3,2,1,0:T(8,128)(2,1)} %all-gather.2.cloned.1.call-done.part_ref, f32[64,16,128]{2,1,0:T(8,128)S(1)} %bitcast.28), custom_call_target="tpu_custom_call" | custom-call | tf_op jit(solution)/shard_map/pallas_call | solution.py:102
  (4 shorter events, 0.1 us)
Async XLA Ops:
  6.5 17.7 %all-to-all-start = ((bf16[4,16,2048]{2,1,0:T(8,128)(2,1)}), bf16[4,16,2048]{2,1,0:T(8,128)(2,1)S(1)}, u32[]{:S(2)}, u32[]{:S(2)}) async-start(bf16[4,16,2048]{2,1,0:T(8,128)(2,1)} %bitcast.34), calls=%async_computation | async-start | bytes 524288 | tf_op jit(solution)/shard_map/all_to_all | solution.py:117
  11.4 138.3 %all-gather.2.cloned.1.call-start = ((), (), s32[]{:S(2)}) async-start(), calls=%async_computation.2 | async-start | bytes 17039360 | tf_op jit(solution)/shard_map/all_gather | solution.py:147
  44.1 2.6 %copy-start = (s32[64,2]{0,1:T(2,128)S(1)}, s32[64,2]{0,1:T(2,128)}, u32[]{:S(2)}) copy-start(s32[64,2]{0,1:T(2,128)} %param.5) | copy-start | bytes 1540
Sparse Core Ops, SparseCore 0:
  46.8 102.7 all-gather.1

commit v4 on v1

--- a/solution.py
+++ b/solution.py
@@ -56,8 +56,8 @@
 ROWS = 32
 
 
-def corr_kernel(owner_ref, part_ref, own_ref, out_hbm, scr, sem):
-    rows_all, freq = part_ref.shape[2], part_ref.shape[3]
+def corr_kernel(owner_ref, part_hbm, own_ref, out_hbm, buf, scr, in_sem, out_sem):
+    rows_all, freq = buf.shape[2], buf.shape[3]
     n_pairs = owner_ref.shape[0]
     n_top = out_hbm.shape[1]
     chunk = min(ROWS, rows_all)
@@ -65,51 +65,64 @@
     even = (row_id % 2) == 0
     sign = jnp.where(even, 1.0, -1.0).astype(jnp.float32)
 
+    def fetch(i, slot):
+        return pltpu.make_async_copy(part_hbm.at[owner_ref[i]], buf.at[slot], in_sem.at[slot])
+
+    fetch(0, 0).start()
+
     def one(i, carry):
         slot = i % 2
         s = i // n_top
         k = i % n_top
-        b = owner_ref[i]
+        fetch(i, slot).wait()
+
+        @pl.when(i + 1 < n_pairs)
+        def _():
+            fetch(i + 1, 1 - slot).start()
 
         @pl.when(i >= 2)
         def _():
-            pltpu.make_async_copy(scr.at[slot], out_hbm.at[0, 0], sem.at[slot]).wait()
+            pltpu.make_async_copy(scr.at[slot], out_hbm.at[0, 0], out_sem.at[slot]).wait()
 
         for c0 in range(0, rows_all, chunk):
             acc1 = jnp.zeros((chunk, freq), jnp.float32)
             acc2 = jnp.zeros((chunk, freq), jnp.float32)
-            for w in range(NW):
-                q = part_ref[b, w, c0 : c0 + chunk, :].astype(jnp.float32)
-                sre = own_ref[s, 2 * w : 2 * w + 1, :].astype(jnp.float32)
-                sim = own_ref[s, 2 * w + 1 : 2 * w + 2, :].astype(jnp.float32)
+            for w in range(buf.shape[1]):
+                q = buf[slot, w, c0 : c0 + chunk, :].astype(jnp.float32)
+                sre = own_ref[s, 2 * w : 2 * w + 1, :]
+                sim = own_ref[s, 2 * w + 1 : 2 * w + 2, :]
                 acc1 = acc1 + q * sre
                 acc2 = acc2 + q * sim
             up = pltpu.roll(acc2, chunk - 1, 0)
             dn = pltpu.roll(acc2, 1, 0)
             res = sign * acc1 + jnp.where(even, up, dn)
             scr[slot, c0 : c0 + chunk, :] = res.astype(scr.dtype)
-        pltpu.make_async_copy(scr.at[slot], out_hbm.at[s, k], sem.at[slot]).start()
+        pltpu.make_async_copy(scr.at[slot], out_hbm.at[s, k], out_sem.at[slot]).start()
         return carry
 
     lax.fori_loop(0, n_pairs, one, 0)
     for back in range(min(2, n_pairs)):
         last = n_pairs - 1 - back
-        pltpu.make_async_copy(scr.at[last % 2], out_hbm.at[0, 0], sem.at[last % 2]).wait()
+        pltpu.make_async_copy(scr.at[last % 2], out_hbm.at[0, 0], out_sem.at[last % 2]).wait()
 
 
 def correlate(owners, part, own, out_shape):
-    rows, freq = part.shape[2], part.shape[3]
+    n_win, rows, freq = part.shape[1], part.shape[2], part.shape[3]
     return pl.pallas_call(
         corr_kernel,
         out_shape=jax.ShapeDtypeStruct(out_shape, jnp.bfloat16),
         in_specs=[
             pl.BlockSpec(memory_space=pltpu.SMEM),
-            pl.BlockSpec(memory_space=pltpu.VMEM),
+            pl.BlockSpec(memory_space=pl.ANY),
             pl.BlockSpec(memory_space=pltpu.VMEM),
         ],
         out_specs=pl.BlockSpec(memory_space=pl.ANY),
-        scratch_shapes=[pltpu.VMEM((2, rows, freq), jnp.bfloat16), pltpu.SemaphoreType.DMA((2,))],
-        compiler_params=pltpu.CompilerParams(vmem_limit_bytes=48 * 1024 * 1024),
+        scratch_shapes=[
+            pltpu.VMEM((2, n_win, rows, freq), jnp.bfloat16),
+            pltpu.VMEM((2, rows, freq), jnp.bfloat16),
+            pltpu.SemaphoreType.DMA((2,)),
+            pltpu.SemaphoreType.DMA((2,)),
+        ],
     )(owners, part, own)
 
 
@@ -145,7 +158,7 @@
     freq = regrouped.shape[3]
     contribution = regrouped.transpose(1, 0, 2, 3).reshape(NW, own_count * 2, freq)
     gathered = lax.all_gather(contribution, "sta", axis=0, tiled=False)
-    own = regrouped.reshape(own_count, NW * 2, freq)
+    own = regrouped.astype(jnp.float32).reshape(own_count, NW * 2, freq)
     out_shape = (own_count, station_owners.shape[1], own_count * 2, freq)
     result = correlate(station_owners.reshape(-1), gathered, own, out_shape)
     return result.reshape(own_count, station_owners.shape[1], own_count, 2, freq)

time: 209 us -> 284 us (1.36); the launches traced: 209 us -> 280 us
  Pallas kernels: 55.2 us -> 126 us
    pallas_call x1, Pallas kernels: 52.2 us -> 123 us  [correlate(): pl.pallas_call(corr_kernel, out_shape=jax.ShapeDtypeStruct(out_shape, jnp...]
  transfers between devices with their start and end apart: 2 -> 2, of which waited for: 1 -> 1; matrix products, arithmetic and copies ran while one was open for 5% -> 4% of each run, Pallas kernels for 1% -> 1%
where the time goes in v4:
time: 284 us; the launch traced here: 280 us
  Pallas kernels  126 us (44%)
  waiting for transfers between devices  101 us (36%)
  between operations  13.5 us (5%)
  local copies, waits for them, and re-layouts  10.4 us (4%)
  other arithmetic  9.93 us (3%)
  blocking collectives  9.57 us (3%)
  starting transfers between devices  4.83 us (2%)
  matrix products  4.1 us (1%)
    pallas_call x1, Pallas kernels, correlate(): pl.pallas_call(corr_kernel, out_shape=jax.ShapeDtypeStruct(out_shape, jnp...  123 us
    all_gather x1, waiting for transfers between devices, shards(): gathered = lax.all_gather(contribution, 'sta', axis=0, tiled=False)  101 us
    all_to_all x1, blocking collectives, shards(): lax.all_to_all(whitened, 'tm', split_axis=3, concat_axis=0, tiled=True)  9.57 us
    another operation x1, other arithmetic  8.54 us
  transfers between devices with their start and end apart: 2, of which 1 were waited for; matrix products, arithmetic and copies ran while one was open for 4% of the time, Pallas kernels for 1%

profile of v4, /device:TPU:1, one launch (start us, length us, event | category | flops | bytes accessed | tf_op | source)
XLA Modules:
  0.0 279.7 jit_solution(8109010470469565317)
XLA Ops:
  6.5 4.8 %all-to-all-start = ((bf16[4,16,2048]{2,1,0:T(8,128)(2,1)}), bf16[4,16,2048]{2,1,0:T(8,128)(2,1)S(1)}, u32[]{:S(2)}, u32[]{:S(2)}) async-start(bf16[4,16,2048]{2,1,0:T(8,128)(2,1)} %bitcast.34), calls=%async_computation | async-start | bytes 524288 | tf_op jit(solution)/shard_map/all_to_all | solution.py:130
  11.4 1.3 pad_convert_fusion
  12.7 3.1 %shard_map.37 = bf16[1024,2048]{1,0:T(8,128)(2,1)} custom-call(f32[1,2048]{1,0:T(1,128)} %bitcast.35), custom_call_target="tpu_custom_call" | custom-call | tf_op jit(solution)/shard_map/pallas_call | solution.py:30
  15.7 8.5 %negate_convert_fusion = (bf16[1024,512]{1,0:T(8,128)(2,1)S(1)}, bf16[1024,512]{1,0:T(8,128)(2,1)S(1)}) fusion(), kind=kLoop, calls=%fused_computation.11 | loop fusion | flops 8912896 | bytes 2097152 | tf_op jit(solution)/shard_map/convert.5
  24.3 0.0 all-to-all-done
  24.3 0.2 copy.31
  24.5 0.1 reshape.32
  24.5 2.9 %convolution_bitcast_fusion = f32[16,8,2048]{2,1,0:T(8,128)S(1)} fusion(bf16[128,1024]{1,0:T(8,128)(2,1)S(1)} %reshape.32, bf16[1024,2048]{1,0:T(8,128)(2,1)} %shard_map.37), kind=kOutput, calls=%fused_computation.3 | convolution fusion | flops 536870912 | bytes 5505024 | tf_op jit(solution)/shard_map/dot_general | solution.py:134
  27.5 0.5 fusion.3
  28.0 0.7 fusion.12
  28.7 0.1 multiply_convert_fusion
  28.8 2.1 copy.32
  30.9 2.2 reshape.39
  33.1 9.6 %all_to_all.34 = bf16[4,2,16384]{2,1,0:T(2,128)(2,1)S(1)} all-to-all(bf16[4,2,16384]{2,1,0:T(2,128)(2,1)S(1)} %reshape.39), channel_id=1, replica_groups=mesh['sta'=64,'tm'=4] {'tm'}, dimensions={0} | all-to-all | bytes 524288 | tf_op jit(solution)/shard_map/all_to_all | solution.py:156
  42.7 1.4 reshape.40
  44.1 0.0 copy-start
  44.1 1.8 copy.34
  45.9 0.7 copy.35
  46.7 0.0 all-gather.2.cloned.1.call-update
  46.7 0.1 copy.30
  46.8 0.7 reshape.31.owner_ref
  47.5 1.1 copy.36
  48.6 101.0 %all-gather.2.cloned.1.call-done.part_hbm = bf16[64,8,128,128]{3,2,1,0:T(8,128)(2,1)} async-done(((bf16[1,8,128,128]{3,2,1,0:T(8,128)(2,1)}), bf16[64,8,128,128]{3,2,1,0:T(8,128)(2,1)}) %all-gather.2.cloned.1.call-update) | async-done | bytes 16777232 | tf_op jit(solution)/shard_map/all_gather | solution.py:160
  149.6 123.2 %shard_map.38 = bf16[64,2,128,128]{3,2,1,0:T(8,128)(2,1)} custom-call(s32[128]{0:T(128)} %reshape.31.owner_ref, bf16[64,8,128,128]{3,2,1,0:T(8,128)(2,1)} %all-gather.2.cloned.1.call-done.part_hbm, f32[64,16,128]{2,1,0:T(8,128)} %bitcast.31), custom_call_target="tpu_custom_call" | custom-call | tf_op jit(solution)/shard_map/pallas_call | solution.py:111
  (4 shorter events, 0.1 us)
Async XLA Ops:
  6.5 17.7 %all-to-all-start = ((bf16[4,16,2048]{2,1,0:T(8,128)(2,1)}), bf16[4,16,2048]{2,1,0:T(8,128)(2,1)S(1)}, u32[]{:S(2)}, u32[]{:S(2)}) async-start(bf16[4,16,2048]{2,1,0:T(8,128)(2,1)} %bitcast.34), calls=%async_computation | async-start | bytes 524288 | tf_op jit(solution)/shard_map/all_to_all | solution.py:130
  11.4 138.3 %all-gather.2.cloned.1.call-start = ((), (), s32[]{:S(2)}) async-start(), calls=%async_computation.2 | async-start | bytes 17039360 | tf_op jit(solution)/shard_map/all_gather | solution.py:160
  44.1 2.6 copy-start
Sparse Core Ops, SparseCore 0:
  46.8 102.7 all-gather.1

commit v5 on v1

--- a/solution.py
+++ b/solution.py
@@ -33,16 +33,19 @@
     )(seed)
 
 
-def transform_table(window_len):
+def transform_table(window_len, quarters):
     bin_count = window_len // 2
-    sample_index = jnp.arange(window_len, dtype=jnp.int32)[:, None]
-    bin_index = jnp.arange(bin_count, dtype=jnp.int32)[None, :]
+    per_quarter = bin_count // quarters
+    sample_index = jnp.arange(window_len, dtype=jnp.int32)[:, None, None]
+    bin_index = (
+        jnp.arange(quarters, dtype=jnp.int32)[None, :, None] * per_quarter
+        + jnp.arange(per_quarter, dtype=jnp.int32)[None, None, :]
+    )
     phase_angle = (sample_index * bin_index % window_len).astype(jnp.float32) * (
         2.0 * math.pi / window_len
     )
-    return jnp.concatenate([jnp.cos(phase_angle), -jnp.sin(phase_angle)], axis=1).astype(
-        jnp.bfloat16
-    )
+    table = jnp.stack([jnp.cos(phase_angle), -jnp.sin(phase_angle)], axis=2)
+    return table.reshape(window_len, 2 * bin_count).astype(jnp.bfloat16)
 
 
 def band_matrix(bin_count, smooth_len):
@@ -80,8 +83,8 @@
             acc2 = jnp.zeros((chunk, freq), jnp.float32)
             for w in range(NW):
                 q = part_ref[b, w, c0 : c0 + chunk, :].astype(jnp.float32)
-                sre = own_ref[s, 2 * w : 2 * w + 1, :].astype(jnp.float32)
-                sim = own_ref[s, 2 * w + 1 : 2 * w + 2, :].astype(jnp.float32)
+                sre = own_ref[w, pl.ds(2 * s, 1), :]
+                sim = own_ref[w, pl.ds(2 * s + 1, 1), :]
                 acc1 = acc1 + q * sre
                 acc2 = acc2 + q * sim
             up = pltpu.roll(acc2, chunk - 1, 0)
@@ -124,10 +127,14 @@
         [jnp.zeros_like(halves[:, :1, WIN:]), halves[:, :-1, WIN:]], axis=1
     )
     filtered = (halves[:, :, :WIN] + carried).astype(jnp.bfloat16).reshape(-1, WIN)
-    spectrum = jnp.dot(filtered, transform_table(WIN), preferred_element_type=jnp.float32)
-    real_part = spectrum[:, :FREQ]
-    imag_part = spectrum[:, FREQ:]
-    power_sum = real_part * real_part + imag_part * imag_part
+    quarters = records.shape[0] // station_count
+    per_quarter = FREQ // quarters
+    spectrum = jnp.dot(
+        filtered, transform_table(WIN, quarters), preferred_element_type=jnp.float32
+    ).reshape(-1, quarters, 2, per_quarter)
+    power_sum = (
+        spectrum[:, :, 0] * spectrum[:, :, 0] + spectrum[:, :, 1] * spectrum[:, :, 1]
+    ).reshape(-1, FREQ)
     smooth = (
         jnp.dot(
             power_sum,
@@ -137,18 +144,19 @@
         )
         / SMOOTH
     )
-    whiten_scale = lax.rsqrt(smooth + 1e-05)
-    whitened = (spectrum.reshape(-1, 2, FREQ) * whiten_scale[:, None, :]).astype(jnp.bfloat16)
-    whitened = whitened.reshape(station_count, NW, 2, FREQ)
-    regrouped = lax.all_to_all(whitened, "tm", split_axis=3, concat_axis=0, tiled=True)
-    own_count = regrouped.shape[0]
-    freq = regrouped.shape[3]
-    contribution = regrouped.transpose(1, 0, 2, 3).reshape(NW, own_count * 2, freq)
+    whiten_scale = lax.rsqrt(smooth + 1e-05).reshape(-1, quarters, 1, per_quarter)
+    whitened = (spectrum * whiten_scale).astype(jnp.bfloat16)
+    whitened = whitened.reshape(station_count, NW, quarters, 2, per_quarter).transpose(
+        2, 1, 0, 3, 4
+    )
+    contribution = lax.all_to_all(whitened, "tm", split_axis=0, concat_axis=2, tiled=True)
+    own_count = contribution.shape[2]
+    contribution = contribution.reshape(NW, own_count * 2, per_quarter)
     gathered = lax.all_gather(contribution, "sta", axis=0, tiled=False)
-    own = regrouped.reshape(own_count, NW * 2, freq)
-    out_shape = (own_count, station_owners.shape[1], own_count * 2, freq)
+    own = contribution.astype(jnp.float32)
+    out_shape = (own_count, station_owners.shape[1], own_count * 2, per_quarter)
     result = correlate(station_owners.reshape(-1), gathered, own, out_shape)
-    return result.reshape(own_count, station_owners.shape[1], own_count, 2, freq)
+    return result.reshape(own_count, station_owners.shape[1], own_count, 2, per_quarter)
 
 
 def solution(mesh):

time: 209 us -> 203 us (0.971)
  local copies, waits for them, and re-layouts: 9.15 us -> 1.99 us
    unnamed x5 -> x3, local copies, waits for them, and re-layouts: 3.72 us -> 0.1 us
    all_to_all x3 -> x0, local copies, waits for them, and re-layouts: 2.16 us -> none  [shards(): lax.all_to_all(whitened, 'tm', split_axis=3, concat_axis=0, tiled=True)]
  transfers between devices with their start and end apart: 2 -> 2, of which waited for: 1 -> 1; matrix products, arithmetic and copies ran while one was open for 5% -> 5% of each run, Pallas kernels for 1% -> 2%
where the time goes in v5:
time: 203 us; the launch traced here: 202 us
  waiting for transfers between devices  102 us (50%)
  Pallas kernels  55 us (27%)
  between operations  13.5 us (7%)
  other arithmetic  10.6 us (5%)
  blocking collectives  9.57 us (5%)
  starting transfers between devices  4.83 us (2%)
  matrix products  4.46 us (2%)
    all_gather x1, waiting for transfers between devices, shards(): gathered = lax.all_gather(contribution, 'sta', axis=0, tiled=False)  102 us
    pallas_call x1, Pallas kernels, correlate(): pl.pallas_call(corr_kernel, out_shape=jax.ShapeDtypeStruct(out_shape, jnp...  51.9 us
    all_to_all x1, blocking collectives, shards(): lax.all_to_all(whitened, 'tm', split_axis=0, concat_axis=2, tiled=True)  9.57 us
    another operation x1, other arithmetic  9.03 us
    all_to_all x1, starting transfers between devices, shards(): lax.all_to_all(records, 'tm', split_axis=0, concat_axis=1, tiled=True)  4.83 us
  transfers between devices with their start and end apart: 2, of which 1 were waited for; matrix products, arithmetic and copies ran while one was open for 5% of the time, Pallas kernels for 2%

profile of v5, /device:TPU:1, one launch (start us, length us, event | category | flops | bytes accessed | tf_op | source)
XLA Modules:
  0.0 202.4 jit_solution(11609498553893612572)
XLA Ops:
  6.5 4.8 %all-to-all-start = ((bf16[4,16,2048]{2,1,0:T(8,128)(2,1)}), bf16[4,16,2048]{2,1,0:T(8,128)(2,1)S(1)}, u32[]{:S(2)}, u32[]{:S(2)}) async-start(bf16[4,16,2048]{2,1,0:T(8,128)(2,1)} %bitcast.48), calls=%async_computation | async-start | bytes 524288 | tf_op jit(solution)/shard_map/all_to_all | solution.py:120
  11.4 0.1 iota_add_fusion
  11.4 1.3 pad_convert_fusion
  12.7 3.1 %shard_map.37 = bf16[1024,2048]{1,0:T(8,128)(2,1)} custom-call(f32[1,2048]{1,0:T(1,128)} %bitcast.50), custom_call_target="tpu_custom_call" | custom-call | tf_op jit(solution)/shard_map/pallas_call | solution.py:30
  15.8 9.0 %cosine_convert_fusion = (bf16[1024,4,1,128]{0,3,2,1:T(8,128)(2,1)S(1)}, bf16[1024,4,1,128]{0,3,2,1:T(8,128)(2,1)S(1)}) fusion(s32[4,128]{1,0:T(4,128)S(1)} %iota_add_fusion), kind=kLoop, calls=%fused_computation.12 | loop fusion | flops 8912896 | bytes 2099200 | tf_op jit(solution)/shard_map/convert.4
  24.8 0.0 all-to-all-done
  24.8 0.2 copy.19
  25.0 0.1 reshape.122
  25.1 2.9 %convolution_bitcast_fusion = f32[16,8,2048]{2,1,0:T(8,128)S(1)} fusion(bf16[128,1024]{1,0:T(8,128)(2,1)S(1)} %reshape.122, bf16[1024,2048]{1,0:T(8,128)(2,1)} %shard_map.37), kind=kOutput, calls=%fused_computation.3 | convolution fusion | flops 536870912 | bytes 5505024 | tf_op jit(solution)/shard_map/dot_general | solution.py:124
  28.1 0.8 fusion.3
  29.0 0.1 copy.20
  29.1 0.7 fusion.11
  29.8 0.0 copy-start
  29.9 0.1 fusion.25
  29.9 0.3 copy.33
  30.2 9.6 %all_to_all.31 = bf16[4,8,16,2,128]{4,3,2,1,0:T(2,128)(2,1)S(1)} all-to-all(bf16[4,8,16,2,128]{4,3,2,1,0:T(2,128)(2,1)S(1)} %bitcast.45), channel_id=1, replica_groups=mesh['sta'=64,'tm'=4] {'tm'}, dimensions={0} | all-to-all | bytes 524288 | tf_op jit(solution)/shard_map/all_to_all | solution.py:152
  39.8 0.2 bitcast_convert_fusion
  39.9 0.7 copy.24
  40.7 0.0 all-gather.2.cloned.1.call-update
  40.7 0.1 copy.18
  40.8 0.1 reshape.121.owner_ref
  41.0 0.3 copy.25
  41.2 102.4 %all-gather.2.cloned.1.call-done.part_ref = bf16[64,8,128,128]{3,2,1,0:T(8,128)(2,1)} async-done(((bf16[1,8,128,128]{3,2,1,0:T(8,128)(2,1)}), bf16[64,8,128,128]{3,2,1,0:T(8,128)(2,1)}) %all-gather.2.cloned.1.call-update) | async-done | bytes 16777232 | tf_op jit(solution)/shard_map/all_gather | solution.py:155
  143.7 51.9 %shard_map.38 = bf16[64,2,128,128]{3,2,1,0:T(8,128)(2,1)} custom-call(s32[128]{0:T(128)S(1)} %reshape.121.owner_ref, bf16[64,8,128,128]{3,2,1,0:T(8,128)(2,1)} %all-gather.2.cloned.1.call-done.part_ref, f32[8,128,128]{2,1,0:T(8,128)S(1)} %bitcast.43), custom_call_target="tpu_custom_call" | custom-call | tf_op jit(solution)/shard_map/pallas_call | solution.py:105
  (6 shorter events, 0.1 us)
Async XLA Ops:
  6.5 18.3 %all-to-all-start = ((bf16[4,16,2048]{2,1,0:T(8,128)(2,1)}), bf16[4,16,2048]{2,1,0:T(8,128)(2,1)S(1)}, u32[]{:S(2)}, u32[]{:S(2)}) async-start(bf16[4,16,2048]{2,1,0:T(8,128)(2,1)} %bitcast.48), calls=%async_computation | async-start | bytes 524288 | tf_op jit(solution)/shard_map/all_to_all | solution.py:120
  11.4 132.3 %all-gather.2.cloned.1.call-start = ((), (), s32[]{:S(2)}) async-start(), calls=%async_computation.2 | async-start | bytes 17039360 | tf_op jit(solution)/shard_map/all_gather | solution.py:155
  29.8 10.9 %copy-start = (s32[64,2]{0,1:T(2,128)S(1)}, s32[64,2]{0,1:T(2,128)}, u32[]{:S(2)}) copy-start(s32[64,2]{0,1:T(2,128)} %param.5) | copy-start | bytes 1540
Sparse Core Ops, SparseCore 0:
  40.8 102.7 all-gather.1

commit v6 on v5

--- a/solution.py
+++ b/solution.py
@@ -1,6 +1,7 @@
 import math
 
 import jax
+import numpy as np
 import jax.numpy as jnp
 from jax import lax
 from jax.experimental import pallas as pl
@@ -36,16 +37,16 @@
 def transform_table(window_len, quarters):
     bin_count = window_len // 2
     per_quarter = bin_count // quarters
-    sample_index = jnp.arange(window_len, dtype=jnp.int32)[:, None, None]
+    sample_index = np.arange(window_len, dtype=np.int64)[:, None, None]
     bin_index = (
-        jnp.arange(quarters, dtype=jnp.int32)[None, :, None] * per_quarter
-        + jnp.arange(per_quarter, dtype=jnp.int32)[None, None, :]
+        np.arange(quarters, dtype=np.int64)[None, :, None] * per_quarter
+        + np.arange(per_quarter, dtype=np.int64)[None, None, :]
     )
-    phase_angle = (sample_index * bin_index % window_len).astype(jnp.float32) * (
+    phase_angle = (sample_index * bin_index % window_len).astype(np.float32) * np.float32(
         2.0 * math.pi / window_len
     )
-    table = jnp.stack([jnp.cos(phase_angle), -jnp.sin(phase_angle)], axis=2)
-    return table.reshape(window_len, 2 * bin_count).astype(jnp.bfloat16)
+    table = np.stack([np.cos(phase_angle), -np.sin(phase_angle)], axis=2)
+    return jnp.asarray(table.reshape(window_len, 2 * bin_count).astype(jnp.bfloat16))
 
 
 def band_matrix(bin_count, smooth_len):

time: 203 us -> 194 us (0.956)
  other arithmetic: 10.6 us -> 1.54 us
    another operation x1 -> x0, other arithmetic: 9.03 us -> none
  transfers between devices with their start and end apart: 2 -> 2, of which waited for: 1 -> 2; matrix products, arithmetic and copies ran while one was open for 5% -> 1% of each run, Pallas kernels for 2% -> 2%
where the time goes in v6:
time: 194 us; the launch traced here: 193 us
  waiting for transfers between devices  104 us (54%)
  Pallas kernels  55 us (28%)
  between operations  13.5 us (7%)
  blocking collectives  8.53 us (4%)
  starting transfers between devices  4.83 us (2%)
  matrix products  4.45 us (2%)
  local copies, waits for them, and re-layouts  1.99 us (1%)
    all_gather x1, waiting for transfers between devices, shards(): gathered = lax.all_gather(contribution, 'sta', axis=0, tiled=False)  102 us
    pallas_call x1, Pallas kernels, correlate(): pl.pallas_call(corr_kernel, out_shape=jax.ShapeDtypeStruct(out_shape, jnp...  51.9 us
    all_to_all x1, blocking collectives, shards(): lax.all_to_all(whitened, 'tm', split_axis=0, concat_axis=2, tiled=True)  8.53 us
    all_to_all x1, starting transfers between devices, shards(): lax.all_to_all(records, 'tm', split_axis=0, concat_axis=1, tiled=True)  4.83 us
  transfers between devices with their start and end apart: 2, of which 2 were waited for; matrix products, arithmetic and copies ran while one was open for 1% of the time, Pallas kernels for 2%

profile of v6, /device:TPU:1, one launch (start us, length us, event | category | flops | bytes accessed | tf_op | source)
XLA Modules:
  0.0 193.5 jit_solution(5911590814802819391)
XLA Ops:
  6.5 4.8 %all-to-all-start = ((bf16[4,16,2048]{2,1,0:T(8,128)(2,1)}), bf16[4,16,2048]{2,1,0:T(8,128)(2,1)S(1)}, u32[]{:S(2)}, u32[]{:S(2)}) async-start(bf16[4,16,2048]{2,1,0:T(8,128)(2,1)} %bitcast.42), calls=%async_computation | async-start | bytes 524288 | tf_op jit(solution)/shard_map/all_to_all | solution.py:121
  11.4 0.0 all-gather.2.cloned.1.call-start
  11.4 1.3 pad_convert_fusion
  12.6 3.1 %shard_map.46 = bf16[1024,2048]{1,0:T(8,128)(2,1)} custom-call(f32[1,2048]{1,0:T(1,128)} %bitcast.44), custom_call_target="tpu_custom_call" | custom-call | tf_op jit(solution)/shard_map/pallas_call | solution.py:31
  15.7 1.2 all-to-all-done
  16.9 0.2 copy.20
  17.1 0.1 reshape.38
  17.2 2.9 %convolution_bitcast_fusion = f32[16,8,2048]{2,1,0:T(8,128)S(1)} fusion(bf16[128,1024]{1,0:T(8,128)(2,1)S(1)} %reshape.38, bf16[1024,2048]{1,0:T(8,128)(2,1)} %shard_map.46), kind=kOutput, calls=%fused_computation | convolution fusion | flops 536870912 | bytes 5505024 | tf_op jit(solution)/shard_map/dot_general | solution.py:125
  20.1 0.0 copy-done
  20.1 0.8 fusion.19
  21.0 0.1 copy.21
  21.2 0.0 copy-start.1
  21.2 0.7 fusion.2
  21.9 0.1 fusion.16
  22.0 0.3 copy.34
  22.3 8.5 %all_to_all.31 = bf16[4,8,16,2,128]{4,3,2,1,0:T(2,128)(2,1)S(1)} all-to-all(bf16[4,8,16,2,128]{4,3,2,1,0:T(2,128)(2,1)S(1)} %bitcast.39), channel_id=1, replica_groups=mesh['sta'=64,'tm'=4] {'tm'}, dimensions={0} | all-to-all | bytes 524288 | tf_op jit(solution)/shard_map/all_to_all | solution.py:153
  30.8 0.2 bitcast_convert_fusion
  31.0 0.7 copy.25
  31.7 0.0 all-gather.2.cloned.1.call-update
  31.8 0.1 copy.19
  31.8 0.1 reshape.37.owner_ref
  32.0 0.3 copy.26
  32.3 102.4 %all-gather.2.cloned.1.call-done.part_ref = bf16[64,8,128,128]{3,2,1,0:T(8,128)(2,1)} async-done(((bf16[1,8,128,128]{3,2,1,0:T(8,128)(2,1)}), bf16[64,8,128,128]{3,2,1,0:T(8,128)(2,1)}) %all-gather.2.cloned.1.call-update) | async-done | bytes 16777232 | tf_op jit(solution)/shard_map/all_gather | solution.py:156
  134.7 51.9 %shard_map.47 = bf16[64,2,128,128]{3,2,1,0:T(8,128)(2,1)} custom-call(s32[128]{0:T(128)S(1)} %reshape.37.owner_ref, bf16[64,8,128,128]{3,2,1,0:T(8,128)(2,1)} %all-gather.2.cloned.1.call-done.part_ref, f32[8,128,128]{2,1,0:T(8,128)S(1)} %bitcast.37), custom_call_target="tpu_custom_call" | custom-call | tf_op jit(solution)/shard_map/pallas_call | solution.py:106
  (5 shorter events, 0.1 us)
Async XLA Ops:
  6.5 10.4 %all-to-all-start = ((bf16[4,16,2048]{2,1,0:T(8,128)(2,1)}), bf16[4,16,2048]{2,1,0:T(8,128)(2,1)S(1)}, u32[]{:S(2)}, u32[]{:S(2)}) async-start(bf16[4,16,2048]{2,1,0:T(8,128)(2,1)} %bitcast.42), calls=%async_computation | async-start | bytes 524288 | tf_op jit(solution)/shard_map/all_to_all | solution.py:121
  11.4 123.3 %all-gather.2.cloned.1.call-start = ((), (), s32[]{:S(2)}) async-start(), calls=%async_computation.2 | async-start | bytes 17039360 | tf_op jit(solution)/shard_map/all_gather | solution.py:156
  15.7 4.4 %copy-start = (bf16[4,2,128,1024]{3,2,1,0:T(8,128)(2,1)S(1)}, bf16[4,2,128,1024]{3,2,1,0:T(8,128)(2,1)}, u32[]{:S(2)}) copy-start(bf16[4,2,128,1024]{3,2,1,0:T(8,128)(2,1)} %constant.37) | copy-start | bytes 6291460
  21.2 10.6 %copy-start.1 = (s32[64,2]{0,1:T(2,128)S(1)}, s32[64,2]{0,1:T(2,128)}, u32[]{:S(2)}) copy-start(s32[64,2]{0,1:T(2,128)} %param.6) | copy-start | bytes 1540
Sparse Core Ops, SparseCore 0:
  31.9 102.7 all-gather.1

commit v7 on v6

--- a/solution.py
+++ b/solution.py
@@ -60,9 +60,10 @@
 ROWS = 32
 
 
-def corr_kernel(owner_ref, part_ref, own_ref, out_hbm, scr, sem):
-    rows_all, freq = part_ref.shape[2], part_ref.shape[3]
-    n_pairs = owner_ref.shape[0]
+def corr_kernel(order_ref, blk_ref, bound_ref, part_ref, own_ref, out_hbm, scr, sem):
+    h = pl.program_id(0)
+    n_half, n_win, rows_all, freq = part_ref.shape
+    n_pairs = order_ref.shape[0]
     n_top = out_hbm.shape[1]
     chunk = min(ROWS, rows_all)
     row_id = lax.broadcasted_iota(jnp.int32, (chunk, freq), 0)
@@ -71,9 +72,10 @@
 
     def one(i, carry):
         slot = i % 2
-        s = i // n_top
-        k = i % n_top
-        b = owner_ref[i]
+        p = order_ref[i]
+        s = p // n_top
+        k = p % n_top
+        b = blk_ref[i] - h * n_half
 
         @pl.when(i >= 2)
         def _():
@@ -82,7 +84,7 @@
         for c0 in range(0, rows_all, chunk):
             acc1 = jnp.zeros((chunk, freq), jnp.float32)
             acc2 = jnp.zeros((chunk, freq), jnp.float32)
-            for w in range(NW):
+            for w in range(n_win):
                 q = part_ref[b, w, c0 : c0 + chunk, :].astype(jnp.float32)
                 sre = own_ref[w, pl.ds(2 * s, 1), :]
                 sim = own_ref[w, pl.ds(2 * s + 1, 1), :]
@@ -95,26 +97,44 @@
         pltpu.make_async_copy(scr.at[slot], out_hbm.at[s, k], sem.at[slot]).start()
         return carry
 
-    lax.fori_loop(0, n_pairs, one, 0)
-    for back in range(min(2, n_pairs)):
-        last = n_pairs - 1 - back
-        pltpu.make_async_copy(scr.at[last % 2], out_hbm.at[0, 0], sem.at[last % 2]).wait()
+    lax.fori_loop(bound_ref[h], bound_ref[h + 1], one, 0)
+
+    @pl.when(h == pl.num_programs(0) - 1)
+    def _():
+        for back in range(min(2, n_pairs)):
+            last = n_pairs - 1 - back
+            pltpu.make_async_copy(scr.at[last % 2], out_hbm.at[0, 0], sem.at[last % 2]).wait()
 
 
 def correlate(owners, part, own, out_shape):
-    rows, freq = part.shape[2], part.shape[3]
+    n_blocks, n_win, rows, freq = part.shape
+    n_half = n_blocks // 2
+    late = (owners >= n_half).astype(jnp.int32)
+    order = jnp.argsort(late, stable=True).astype(jnp.int32)
+    blk = owners[order].astype(jnp.int32)
+    n_early = owners.shape[0] - jnp.sum(late)
+    bounds = jnp.stack([jnp.zeros((), jnp.int32), n_early.astype(jnp.int32), jnp.full((), owners.shape[0], jnp.int32)])
+    grid_spec = pltpu.PrefetchScalarGridSpec(
+        num_scalar_prefetch=3,
+        grid=(2,),
+        in_specs=[
+            pl.BlockSpec((n_half, n_win, rows, freq), lambda h, *_: (h, 0, 0, 0)),
+            pl.BlockSpec(own.shape, lambda h, *_: (0, 0, 0)),
+        ],
+        out_specs=pl.BlockSpec(memory_space=pl.ANY),
+        scratch_shapes=[
+            pltpu.VMEM((2, rows, freq), jnp.bfloat16),
+            pltpu.SemaphoreType.DMA((2,)),
+        ],
+    )
     return pl.pallas_call(
         corr_kernel,
         out_shape=jax.ShapeDtypeStruct(out_shape, jnp.bfloat16),
-        in_specs=[
-            pl.BlockSpec(memory_space=pltpu.SMEM),
-            pl.BlockSpec(memory_space=pltpu.VMEM),
-            pl.BlockSpec(memory_space=pltpu.VMEM),
-        ],
-        out_specs=pl.BlockSpec(memory_space=pl.ANY),
-        scratch_shapes=[pltpu.VMEM((2, rows, freq), jnp.bfloat16), pltpu.SemaphoreType.DMA((2,))],
-        compiler_params=pltpu.CompilerParams(vmem_limit_bytes=48 * 1024 * 1024),
-    )(owners, part, own)
+        grid_spec=grid_spec,
+        compiler_params=pltpu.CompilerParams(
+            dimension_semantics=("arbitrary",), vmem_limit_bytes=48 * 1024 * 1024
+        ),
+    )(order, blk, bounds, part, own)
 
 
 def shards(records, band_taps, station_owners):

time: 194 us -> 192 us (0.990)
  waiting for transfers between devices: 104 us -> 98.6 us
  other arithmetic: 1.54 us -> 4.79 us
    all_gather x1, waiting for transfers between devices: 102 us -> 97.4 us  [shards(): gathered = lax.all_gather(contribution, 'sta', axis=0, tiled=False)]
    sort x0 -> x1, other arithmetic: none -> 2.53 us  [correlate(): order = jnp.argsort(late, stable=True).astype(jnp.int32)]
  transfers between devices with their start and end apart: 2 -> 2, of which waited for: 2 -> 2; matrix products, arithmetic and copies ran while one was open for 1% -> 3% of each run, Pallas kernels for 2% -> 2%
where the time goes in v7:
time: 192 us
  waiting for transfers between devices  98.6 us (51%)
  Pallas kernels  53.1 us (28%)
  between operations  14.1 us (7%)
  blocking collectives  8.53 us (4%)
  starting transfers between devices  4.83 us (3%)
  other arithmetic  4.79 us (2%)
  matrix products  4.45 us (2%)
  local copies, waits for them, and re-layouts  3.22 us (2%)
    all_gather x1, waiting for transfers between devices, shards(): gathered = lax.all_gather(contribution, 'sta', axis=0, tiled=False)  97.4 us
    pallas_call x1, Pallas kernels, correlate(): pl.pallas_call(corr_kernel, out_shape=jax.ShapeDtypeStruct(out_shape, jnp...  50.1 us
    all_to_all x1, blocking collectives, shards(): lax.all_to_all(whitened, 'tm', split_axis=0, concat_axis=2, tiled=True)  8.53 us
    all_to_all x1, starting transfers between devices, shards(): lax.all_to_all(records, 'tm', split_axis=0, concat_axis=1, tiled=True)  4.83 us
  transfers between devices with their start and end apart: 2, of which 2 were waited for; matrix products, arithmetic and copies ran while one was open for 3% of the time, Pallas kernels for 2%

profile of v7, /device:TPU:1, one launch (start us, length us, event | category | flops | bytes accessed | tf_op | source)
XLA Modules:
  0.0 191.7 jit_solution(5800237826939033874)
XLA Ops:
  6.5 4.8 %all-to-all-start = ((bf16[4,16,2048]{2,1,0:T(8,128)(2,1)}), bf16[4,16,2048]{2,1,0:T(8,128)(2,1)S(1)}, u32[]{:S(2)}, u32[]{:S(2)}) async-start(bf16[4,16,2048]{2,1,0:T(8,128)(2,1)} %bitcast.43), calls=%async_computation | async-start | bytes 524288 | tf_op jit(solution)/shard_map/all_to_all | solution.py:141
  11.4 1.3 pad_convert_fusion
  12.6 3.1 %shard_map.46 = bf16[1024,2048]{1,0:T(8,128)(2,1)} custom-call(f32[1,2048]{1,0:T(1,128)} %bitcast.45), custom_call_target="tpu_custom_call" | custom-call | tf_op jit(solution)/shard_map/pallas_call | solution.py:31
  15.7 1.2 all-to-all-done
  16.9 0.2 copy.20
  17.1 0.1 reshape.38
  17.2 2.9 %convolution_bitcast_fusion = f32[16,8,2048]{2,1,0:T(8,128)S(1)} fusion(bf16[128,1024]{1,0:T(8,128)(2,1)S(1)} %reshape.38, bf16[1024,2048]{1,0:T(8,128)(2,1)} %shard_map.46), kind=kOutput, calls=%fused_computation.1 | convolution fusion | flops 536870912 | bytes 5505024 | tf_op jit(solution)/shard_map/dot_general | solution.py:145
  20.1 0.8 fusion.19
  21.0 0.1 copy.21
  21.2 0.7 fusion.2
  21.9 0.1 fusion.16
  22.0 0.3 copy.34
  22.3 8.5 %all_to_all.31 = bf16[4,8,16,2,128]{4,3,2,1,0:T(2,128)(2,1)S(1)} all-to-all(bf16[4,8,16,2,128]{4,3,2,1,0:T(2,128)(2,1)S(1)} %bitcast.40), channel_id=1, replica_groups=mesh['sta'=64,'tm'=4] {'tm'}, dimensions={0} | all-to-all | bytes 524288 | tf_op jit(solution)/shard_map/all_to_all | solution.py:173
  30.8 0.2 bitcast_convert_fusion
  31.0 0.7 copy.25
  31.8 0.1 copy.19
  31.8 0.1 reshape.37
  32.0 2.5 %sort.17 = (s32[128]{0:T(128)}, s32[128]{0:T(128)S(1)}) sort(s32[128]{0:T(128)S(1)} %compare_convert_fusion.1, s32[128]{0:T(128)S(1)} %iota.11), dimensions={0}, to_apply=%region_0.1 | sort | flops 896 | bytes 2048 | tf_op jit(solution)/shard_map/jit(argsort)/sort | solution.py:113
  34.6 1.2 gather_fusion
  35.8 0.6 fusion.21
  37.0 0.1 pad_add_fusion.bound_ref
  37.1 0.3 copy.26
  37.3 97.4 %all-gather.2.cloned.1.call-done.part_ref = bf16[64,8,128,128]{3,2,1,0:T(8,128)(2,1)} async-done(((bf16[1,8,128,128]{3,2,1,0:T(8,128)(2,1)}), bf16[64,8,128,128]{3,2,1,0:T(8,128)(2,1)}) %all-gather.2.cloned.1.call-update) | async-done | bytes 16777232 | tf_op jit(solution)/shard_map/all_gather | solution.py:176
  134.7 50.1 %shard_map.47 = bf16[64,2,128,128]{3,2,1,0:T(8,128)(2,1)} custom-call(s32[128]{0:T(128)S(1)} %get-tuple-element.6.order_ref, s32[128]{0:T(128)S(1)} %gather_fusion, s32[3]{0:T(128)S(1)} %pad_add_fusion.bound_ref, bf16[64,8,128,128]{3,2,1,0:T(8,128)(2,1)} %all-gather.2.cloned.1.call-done.part_ref, f32[8,128,128]{2,1,0:T(8,128)S(1)} %bitcast.38), custom_call_target="tpu_custom_call" | custom-call | tf_op jit(solution)/shard_map/pallas_call | solution.py:130
  (13 shorter events, 0.1 us)
Async XLA Ops:
  6.5 10.4 %all-to-all-start = ((bf16[4,16,2048]{2,1,0:T(8,128)(2,1)}), bf16[4,16,2048]{2,1,0:T(8,128)(2,1)S(1)}, u32[]{:S(2)}, u32[]{:S(2)}) async-start(bf16[4,16,2048]{2,1,0:T(8,128)(2,1)} %bitcast.43), calls=%async_computation | async-start | bytes 524288 | tf_op jit(solution)/shard_map/all_to_all | solution.py:141
  11.4 123.4 %all-gather.2.cloned.1.call-start = ((), (), s32[]{:S(2)}) async-start(), calls=%async_computation.2 | async-start | bytes 17039360 | tf_op jit(solution)/shard_map/all_gather | solution.py:176
  15.7 4.4 %copy-start = (bf16[4,2,128,1024]{3,2,1,0:T(8,128)(2,1)S(1)}, bf16[4,2,128,1024]{3,2,1,0:T(8,128)(2,1)}, u32[]{:S(2)}) copy-start(bf16[4,2,128,1024]{3,2,1,0:T(8,128)(2,1)} %constant.47) | copy-start | bytes 6291460
  21.2 10.6 %copy-start.1 = (s32[64,2]{0,1:T(2,128)S(1)}, s32[64,2]{0,1:T(2,128)}, u32[]{:S(2)}) copy-start(s32[64,2]{0,1:T(2,128)} %param.6) | copy-start | bytes 1540
Sparse Core Ops, SparseCore 0:
  31.9 102.8 all-gather.1

commit v8 on v7

--- a/solution.py
+++ b/solution.py
@@ -60,15 +60,13 @@
 ROWS = 32
 
 
-def corr_kernel(order_ref, blk_ref, bound_ref, part_ref, own_ref, out_hbm, scr, sem):
+def corr_kernel(order_ref, blk_ref, bound_ref, part_ref, own_ref, out_hbm, scr, wide, sem):
     h = pl.program_id(0)
     n_half, n_win, rows_all, freq = part_ref.shape
     n_pairs = order_ref.shape[0]
     n_top = out_hbm.shape[1]
-    chunk = min(ROWS, rows_all)
-    row_id = lax.broadcasted_iota(jnp.int32, (chunk, freq), 0)
-    even = (row_id % 2) == 0
-    sign = jnp.where(even, 1.0, -1.0).astype(jnp.float32)
+    half = rows_all // 2
+    chunk = min(ROWS, half)
 
     def one(i, carry):
         slot = i % 2
@@ -81,19 +79,19 @@
         def _():
             pltpu.make_async_copy(scr.at[slot], out_hbm.at[0, 0], sem.at[slot]).wait()
 
-        for c0 in range(0, rows_all, chunk):
-            acc1 = jnp.zeros((chunk, freq), jnp.float32)
-            acc2 = jnp.zeros((chunk, freq), jnp.float32)
+        for c0 in range(0, half, chunk):
+            real_sum = jnp.zeros((chunk, freq), jnp.float32)
+            imag_sum = jnp.zeros((chunk, freq), jnp.float32)
             for w in range(n_win):
-                q = part_ref[b, w, c0 : c0 + chunk, :].astype(jnp.float32)
-                sre = own_ref[w, pl.ds(2 * s, 1), :]
-                sim = own_ref[w, pl.ds(2 * s + 1, 1), :]
-                acc1 = acc1 + q * sre
-                acc2 = acc2 + q * sim
-            up = pltpu.roll(acc2, chunk - 1, 0)
-            dn = pltpu.roll(acc2, 1, 0)
-            res = sign * acc1 + jnp.where(even, up, dn)
-            scr[slot, c0 : c0 + chunk, :] = res.astype(scr.dtype)
+                par_re = part_ref[b, w, c0 : c0 + chunk, :].astype(jnp.float32)
+                par_im = part_ref[b, w, half + c0 : half + c0 + chunk, :].astype(jnp.float32)
+                sig_re = own_ref[w, pl.ds(s, 1), :]
+                sig_im = own_ref[w, pl.ds(half + s, 1), :]
+                real_sum = real_sum + par_re * sig_re + par_im * sig_im
+                imag_sum = imag_sum + par_re * sig_im - par_im * sig_re
+            wide[pl.ds(2 * c0, chunk, stride=2), :] = real_sum
+            wide[pl.ds(2 * c0 + 1, chunk, stride=2), :] = imag_sum
+        scr[slot] = wide[...].astype(scr.dtype)
         pltpu.make_async_copy(scr.at[slot], out_hbm.at[s, k], sem.at[slot]).start()
         return carry
 
@@ -124,6 +122,7 @@
         out_specs=pl.BlockSpec(memory_space=pl.ANY),
         scratch_shapes=[
             pltpu.VMEM((2, rows, freq), jnp.bfloat16),
+            pltpu.VMEM((rows, freq), jnp.float32),
             pltpu.SemaphoreType.DMA((2,)),
         ],
     )
@@ -168,10 +167,10 @@
     whiten_scale = lax.rsqrt(smooth + 1e-05).reshape(-1, quarters, 1, per_quarter)
     whitened = (spectrum * whiten_scale).astype(jnp.bfloat16)
     whitened = whitened.reshape(station_count, NW, quarters, 2, per_quarter).transpose(
-        2, 1, 0, 3, 4
+        2, 1, 3, 0, 4
     )
-    contribution = lax.all_to_all(whitened, "tm", split_axis=0, concat_axis=2, tiled=True)
-    own_count = contribution.shape[2]
+    contribution = lax.all_to_all(whitened, "tm", split_axis=0, concat_axis=3, tiled=True)
+    own_count = contribution.shape[3]
     contribution = contribution.reshape(NW, own_count * 2, per_quarter)
     gathered = lax.all_gather(contribution, "sta", axis=0, tiled=False)
     own = contribution.astype(jnp.float32)

time: 192 us -> 191 us (level)
  transfers between devices with their start and end apart: 2 -> 2, of which waited for: 2 -> 2; matrix products, arithmetic and copies ran while one was open for 3% -> 4% of each run, Pallas kernels for 2% -> 2%
where the time goes in v8:
time: 191 us; the launch traced here: 190 us
  waiting for transfers between devices  97.9 us (51%)
  Pallas kernels  52.3 us (27%)
  between operations  14.1 us (7%)
  blocking collectives  8.53 us (4%)
  other arithmetic  5.6 us (3%)
  starting transfers between devices  4.83 us (3%)
  matrix products  4.45 us (2%)
  local copies, waits for them, and re-layouts  2.7 us (1%)
    all_gather x1, waiting for transfers between devices, shards(): gathered = lax.all_gather(contribution, 'sta', axis=0, tiled=False)  96.7 us
    pallas_call x1, Pallas kernels, correlate(): pl.pallas_call(corr_kernel, out_shape=jax.ShapeDtypeStruct(out_shape, jnp...  49.2 us
    all_to_all x1, blocking collectives, shards(): lax.all_to_all(whitened, 'tm', split_axis=0, concat_axis=3, tiled=True)  8.53 us
    all_to_all x1, starting transfers between devices, shards(): lax.all_to_all(records, 'tm', split_axis=0, concat_axis=1, tiled=True)  4.83 us
  transfers between devices with their start and end apart: 2, of which 2 were waited for; matrix products, arithmetic and copies ran while one was open for 4% of the time, Pallas kernels for 2%

profile of v8, /device:TPU:1, one launch (start us, length us, event | category | flops | bytes accessed | tf_op | source)
XLA Modules:
  0.0 190.4 jit_solution(10097678488294365279)
XLA Ops:
  6.5 4.8 %all-to-all-start = ((bf16[4,16,2048]{2,1,0:T(8,128)(2,1)}), bf16[4,16,2048]{2,1,0:T(8,128)(2,1)S(1)}, u32[]{:S(2)}, u32[]{:S(2)}) async-start(bf16[4,16,2048]{2,1,0:T(8,128)(2,1)} %bitcast.44), calls=%async_computation | async-start | bytes 524288 | tf_op jit(solution)/shard_map/all_to_all | solution.py:140
  11.4 1.3 pad_convert_fusion
  12.6 3.1 %shard_map.46 = bf16[1024,2048]{1,0:T(8,128)(2,1)} custom-call(f32[1,2048]{1,0:T(1,128)} %bitcast.46), custom_call_target="tpu_custom_call" | custom-call | tf_op jit(solution)/shard_map/pallas_call | solution.py:31
  15.7 1.2 all-to-all-done
  16.9 0.2 copy.20
  17.1 0.1 reshape.38
  17.2 2.9 %convolution_bitcast_fusion = f32[16,8,2048]{2,1,0:T(8,128)S(1)} fusion(bf16[128,1024]{1,0:T(8,128)(2,1)S(1)} %reshape.38, bf16[1024,2048]{1,0:T(8,128)(2,1)} %shard_map.46), kind=kOutput, calls=%fused_computation.1 | convolution fusion | flops 536870912 | bytes 5505024 | tf_op jit(solution)/shard_map/dot_general | solution.py:144
  20.1 0.8 fusion.19
  21.0 0.1 copy.21
  21.2 0.0 copy-start.1
  21.2 0.7 fusion.2
  21.9 0.1 fusion.16
  22.0 8.5 %all_to_all.31 = bf16[4,8,2,16,128]{4,3,2,1,0:T(8,128)(2,1)S(1)} all-to-all(bf16[4,8,2,16,128]{4,3,2,1,0:T(8,128)(2,1)S(1)} %bitcast.42), channel_id=1, replica_groups=mesh['sta'=64,'tm'=4] {'tm'}, dimensions={0} | all-to-all | bytes 524288 | tf_op jit(solution)/shard_map/all_to_all | solution.py:172
  30.6 0.7 copy.24
  31.3 0.0 all-gather.2.cloned.1.call-update
  31.3 0.1 copy.19
  31.4 0.1 reshape.37
  31.6 2.5 %sort.17 = (s32[128]{0:T(128)}, s32[128]{0:T(128)S(1)}) sort(s32[128]{0:T(128)S(1)} %compare_convert_fusion.1, s32[128]{0:T(128)S(1)} %iota.11), dimensions={0}, to_apply=%region_0.1 | sort | flops 896 | bytes 2048 | tf_op jit(solution)/shard_map/jit(argsort)/sort | solution.py:111
  34.1 1.2 gather_fusion
  35.4 0.6 fusion.21
  36.6 0.1 pad_add_fusion.bound_ref
  36.6 1.0 bitcast_convert_fusion.own_ref
  37.6 96.7 %all-gather.2.cloned.1.call-done.part_ref = bf16[64,8,128,128]{3,2,1,0:T(8,128)(2,1)} async-done(((bf16[1,8,128,128]{3,2,1,0:T(8,128)(2,1)}), bf16[64,8,128,128]{3,2,1,0:T(8,128)(2,1)}) %all-gather.2.cloned.1.call-update) | async-done | bytes 16777232 | tf_op jit(solution)/shard_map/all_gather | solution.py:175
  134.3 49.2 %shard_map.47 = bf16[64,2,128,128]{3,2,1,0:T(8,128)(2,1)} custom-call(s32[128]{0:T(128)S(1)} %get-tuple-element.6.order_ref, s32[128]{0:T(128)S(1)} %gather_fusion, s32[3]{0:T(128)S(1)} %pad_add_fusion.bound_ref, bf16[64,8,128,128]{3,2,1,0:T(8,128)(2,1)} %all-gather.2.cloned.1.call-done.part_ref, f32[8,128,128]{2,1,0:T(8,128)S(1)} %bitcast_convert_fusion.own_ref), custom_call_target="tpu_custom_call" | custom-call | tf_op jit(solution)/shard_map/pallas_call | solution.py:129
  (12 shorter events, 0.2 us)
Async XLA Ops:
  6.5 10.4 %all-to-all-start = ((bf16[4,16,2048]{2,1,0:T(8,128)(2,1)}), bf16[4,16,2048]{2,1,0:T(8,128)(2,1)S(1)}, u32[]{:S(2)}, u32[]{:S(2)}) async-start(bf16[4,16,2048]{2,1,0:T(8,128)(2,1)} %bitcast.44), calls=%async_computation | async-start | bytes 524288 | tf_op jit(solution)/shard_map/all_to_all | solution.py:140
  11.4 122.9 %all-gather.2.cloned.1.call-start = ((), (), s32[]{:S(2)}) async-start(), calls=%async_computation.2 | async-start | bytes 17039360 | tf_op jit(solution)/shard_map/all_gather | solution.py:175
  15.7 4.4 %copy-start = (bf16[4,2,128,1024]{3,2,1,0:T(8,128)(2,1)S(1)}, bf16[4,2,128,1024]{3,2,1,0:T(8,128)(2,1)}, u32[]{:S(2)}) copy-start(bf16[4,2,128,1024]{3,2,1,0:T(8,128)(2,1)} %constant.47) | copy-start | bytes 6291460
  21.2 10.2 %copy-start.1 = (s32[64,2]{0,1:T(2,128)S(1)}, s32[64,2]{0,1:T(2,128)}, u32[]{:S(2)}) copy-start(s32[64,2]{0,1:T(2,128)} %param.6) | copy-start | bytes 1540
Sparse Core Ops, SparseCore 0:
  31.4 102.8 all-gather.1

commit v9 on v8

--- a/solution.py
+++ b/solution.py
@@ -104,17 +104,20 @@
             pltpu.make_async_copy(scr.at[last % 2], out_hbm.at[0, 0], sem.at[last % 2]).wait()
 
 
-def correlate(owners, part, own, out_shape):
+def correlate(owners, part, own, out_shape, n_parts=4):
     n_blocks, n_win, rows, freq = part.shape
-    n_half = n_blocks // 2
-    late = (owners >= n_half).astype(jnp.int32)
-    order = jnp.argsort(late, stable=True).astype(jnp.int32)
+    n_half = n_blocks // n_parts
+    part_of = (owners // n_half).astype(jnp.int32)
+    order = jnp.argsort(part_of, stable=True).astype(jnp.int32)
     blk = owners[order].astype(jnp.int32)
-    n_early = owners.shape[0] - jnp.sum(late)
-    bounds = jnp.stack([jnp.zeros((), jnp.int32), n_early.astype(jnp.int32), jnp.full((), owners.shape[0], jnp.int32)])
+    counts = jnp.sum(
+        (part_of[None, :] == jnp.arange(n_parts, dtype=jnp.int32)[:, None]).astype(jnp.int32),
+        axis=1,
+    )
+    bounds = jnp.concatenate([jnp.zeros((1,), jnp.int32), jnp.cumsum(counts).astype(jnp.int32)])
     grid_spec = pltpu.PrefetchScalarGridSpec(
         num_scalar_prefetch=3,
-        grid=(2,),
+        grid=(n_parts,),
         in_specs=[
             pl.BlockSpec((n_half, n_win, rows, freq), lambda h, *_: (h, 0, 0, 0)),
             pl.BlockSpec(own.shape, lambda h, *_: (0, 0, 0)),

time: 191 us -> 190 us (level)
  no operation moved by 1% of the time
where the time goes in v9:
time: 190 us; the launch traced here: 189 us
  waiting for transfers between devices  98.8 us (52%)
  Pallas kernels  51.1 us (27%)
  between operations  13.5 us (7%)
  blocking collectives  8.53 us (4%)
  other arithmetic  5.27 us (3%)
  starting transfers between devices  4.83 us (3%)
  matrix products  4.45 us (2%)
  local copies, waits for them, and re-layouts  2.7 us (1%)
    all_gather x1, waiting for transfers between devices, shards(): gathered = lax.all_gather(contribution, 'sta', axis=0, tiled=False)  97.6 us
    pallas_call x1, Pallas kernels, correlate(): pl.pallas_call(corr_kernel, out_shape=jax.ShapeDtypeStruct(out_shape, jnp...  48.1 us
    all_to_all x1, blocking collectives, shards(): lax.all_to_all(whitened, 'tm', split_axis=0, concat_axis=3, tiled=True)  8.53 us
    all_to_all x1, starting transfers between devices, shards(): lax.all_to_all(records, 'tm', split_axis=0, concat_axis=1, tiled=True)  4.83 us
  transfers between devices with their start and end apart: 2, of which 2 were waited for; matrix products, arithmetic and copies ran while one was open for 4% of the time, Pallas kernels for 2%

profile of v9, /device:TPU:1, one launch (start us, length us, event | category | flops | bytes accessed | tf_op | source)
XLA Modules:
  0.0 189.2 jit_solution(8771669267116117063)
XLA Ops:
  6.5 4.8 %all-to-all-start = ((bf16[4,16,2048]{2,1,0:T(8,128)(2,1)}), bf16[4,16,2048]{2,1,0:T(8,128)(2,1)S(1)}, u32[]{:S(2)}, u32[]{:S(2)}) async-start(bf16[4,16,2048]{2,1,0:T(8,128)(2,1)} %bitcast.45), calls=%async_computation | async-start | bytes 524288 | tf_op jit(solution)/shard_map/all_to_all | solution.py:143
  11.4 1.3 pad_convert_fusion
  12.6 3.1 %shard_map.46 = bf16[1024,2048]{1,0:T(8,128)(2,1)} custom-call(f32[1,2048]{1,0:T(1,128)} %bitcast.47), custom_call_target="tpu_custom_call" | custom-call | tf_op jit(solution)/shard_map/pallas_call | solution.py:31
  15.7 1.2 all-to-all-done
  16.9 0.2 copy.26
  17.1 0.1 reshape.94
  17.2 2.9 %convolution_bitcast_fusion = f32[16,8,2048]{2,1,0:T(8,128)S(1)} fusion(bf16[128,1024]{1,0:T(8,128)(2,1)S(1)} %reshape.94, bf16[1024,2048]{1,0:T(8,128)(2,1)} %shard_map.46), kind=kOutput, calls=%fused_computation.1 | convolution fusion | flops 536870912 | bytes 5505024 | tf_op jit(solution)/shard_map/dot_general | solution.py:147
  20.1 0.8 fusion.19
  21.0 0.1 copy.27
  21.2 0.7 fusion.2
  21.9 0.1 fusion.16
  22.0 8.5 %all_to_all.31 = bf16[4,8,2,16,128]{4,3,2,1,0:T(8,128)(2,1)S(1)} all-to-all(bf16[4,8,2,16,128]{4,3,2,1,0:T(8,128)(2,1)S(1)} %bitcast.43), channel_id=1, replica_groups=mesh['sta'=64,'tm'=4] {'tm'}, dimensions={0} | all-to-all | bytes 524288 | tf_op jit(solution)/shard_map/all_to_all | solution.py:175
  30.6 0.7 copy.30
  31.3 0.0 all-gather.2.cloned.1.call-update
  31.3 0.1 copy.25
  31.4 0.1 reshape.91
  31.6 2.5 %sort.17 = (s32[128]{0:T(128)}, s32[128]{0:T(128)S(1)}) sort(s32[128]{0:T(128)S(1)} %and_select_fusion, s32[128]{0:T(128)S(1)} %iota.15), dimensions={0}, to_apply=%region_0.1 | sort | flops 896 | bytes 2048 | tf_op jit(solution)/shard_map/jit(argsort)/sort | solution.py:111
  34.1 1.2 gather_fusion
  35.4 0.1 convert_reduce_fusion
  35.5 0.2 reduce-window.9
  35.7 0.1 pad_add_fusion.bound_ref
  35.7 1.0 bitcast_convert_fusion.own_ref
  36.7 97.6 %all-gather.2.cloned.1.call-done.part_ref = bf16[64,8,128,128]{3,2,1,0:T(8,128)(2,1)} async-done(((bf16[1,8,128,128]{3,2,1,0:T(8,128)(2,1)}), bf16[64,8,128,128]{3,2,1,0:T(8,128)(2,1)}) %all-gather.2.cloned.1.call-update) | async-done | bytes 16777232 | tf_op jit(solution)/shard_map/all_gather | solution.py:178
  134.3 48.1 %shard_map.47 = bf16[64,2,128,128]{3,2,1,0:T(8,128)(2,1)} custom-call(s32[128]{0:T(128)S(1)} %get-tuple-element.6.order_ref, s32[128]{0:T(128)S(1)} %gather_fusion, s32[5]{0:T(128)S(1)} %pad_add_fusion.bound_ref, bf16[64,8,128,128]{3,2,1,0:T(8,128)(2,1)} %all-gather.2.cloned.1.call-done.part_ref, f32[8,128,128]{2,1,0:T(8,128)S(1)} %bitcast_convert_fusion.own_ref), custom_call_target="tpu_custom_call" | custom-call | tf_op jit(solution)/shard_map/pallas_call | solution.py:132
  (13 shorter events, 0.2 us)
Async XLA Ops:
  6.5 10.4 %all-to-all-start = ((bf16[4,16,2048]{2,1,0:T(8,128)(2,1)}), bf16[4,16,2048]{2,1,0:T(8,128)(2,1)S(1)}, u32[]{:S(2)}, u32[]{:S(2)}) async-start(bf16[4,16,2048]{2,1,0:T(8,128)(2,1)} %bitcast.45), calls=%async_computation | async-start | bytes 524288 | tf_op jit(solution)/shard_map/all_to_all | solution.py:143
  11.4 122.9 %all-gather.2.cloned.1.call-start = ((), (), s32[]{:S(2)}) async-start(), calls=%async_computation.2 | async-start | bytes 17039360 | tf_op jit(solution)/shard_map/all_gather | solution.py:178
  15.7 4.4 %copy-start = (bf16[4,2,128,1024]{3,2,1,0:T(8,128)(2,1)S(1)}, bf16[4,2,128,1024]{3,2,1,0:T(8,128)(2,1)}, u32[]{:S(2)}) copy-start(bf16[4,2,128,1024]{3,2,1,0:T(8,128)(2,1)} %constant.61) | copy-start | bytes 6291460
  21.2 10.2 %copy-start.1 = (s32[64,2]{0,1:T(2,128)S(1)}, s32[64,2]{0,1:T(2,128)}, u32[]{:S(2)}) copy-start(s32[64,2]{0,1:T(2,128)} %param.6) | copy-start | bytes 1540
Sparse Core Ops, SparseCore 0:
  31.4 102.8 all-gather.1

commit v10 on v9

--- a/solution.py
+++ b/solution.py
@@ -104,7 +104,7 @@
             pltpu.make_async_copy(scr.at[last % 2], out_hbm.at[0, 0], sem.at[last % 2]).wait()
 
 
-def correlate(owners, part, own, out_shape, n_parts=4):
+def correlate(owners, part, own, out_shape, n_parts=8):
     n_blocks, n_win, rows, freq = part.shape
     n_half = n_blocks // n_parts
     part_of = (owners // n_half).astype(jnp.int32)

time: 190 us -> 189 us (level)
  no operation moved by 1% of the time
where the time goes in v10:
time: 189 us
  waiting for transfers between devices  98.8 us (52%)
  Pallas kernels  50.5 us (27%)
  between operations  13.5 us (7%)
  blocking collectives  8.53 us (5%)
  other arithmetic  5.28 us (3%)
  starting transfers between devices  4.83 us (3%)
  matrix products  4.45 us (2%)
  local copies, waits for them, and re-layouts  2.7 us (1%)
    all_gather x1, waiting for transfers between devices, shards(): gathered = lax.all_gather(contribution, 'sta', axis=0, tiled=False)  97.6 us
    pallas_call x1, Pallas kernels, correlate(): pl.pallas_call(corr_kernel, out_shape=jax.ShapeDtypeStruct(out_shape, jnp...  47.5 us
    all_to_all x1, blocking collectives, shards(): lax.all_to_all(whitened, 'tm', split_axis=0, concat_axis=3, tiled=True)  8.53 us
    all_to_all x1, starting transfers between devices, shards(): lax.all_to_all(records, 'tm', split_axis=0, concat_axis=1, tiled=True)  4.83 us
  transfers between devices with their start and end apart: 2, of which 2 were waited for; matrix products, arithmetic and copies ran while one was open for 4% of the time, Pallas kernels for 2%

profile of v10, /device:TPU:1, one launch (start us, length us, event | category | flops | bytes accessed | tf_op | source)
XLA Modules:
  0.0 188.6 jit_solution(16349213446379450087)
XLA Ops:
  6.5 4.8 %all-to-all-start = ((bf16[4,16,2048]{2,1,0:T(8,128)(2,1)}), bf16[4,16,2048]{2,1,0:T(8,128)(2,1)S(1)}, u32[]{:S(2)}, u32[]{:S(2)}) async-start(bf16[4,16,2048]{2,1,0:T(8,128)(2,1)} %bitcast.45), calls=%async_computation | async-start | bytes 524288 | tf_op jit(solution)/shard_map/all_to_all | solution.py:143
  11.4 1.3 pad_convert_fusion
  12.6 3.1 %shard_map.46 = bf16[1024,2048]{1,0:T(8,128)(2,1)} custom-call(f32[1,2048]{1,0:T(1,128)} %bitcast.47), custom_call_target="tpu_custom_call" | custom-call | tf_op jit(solution)/shard_map/pallas_call | solution.py:31
  15.7 1.2 all-to-all-done
  16.9 0.2 copy.26
  17.1 0.1 reshape.94
  17.2 2.9 %convolution_bitcast_fusion = f32[16,8,2048]{2,1,0:T(8,128)S(1)} fusion(bf16[128,1024]{1,0:T(8,128)(2,1)S(1)} %reshape.94, bf16[1024,2048]{1,0:T(8,128)(2,1)} %shard_map.46), kind=kOutput, calls=%fused_computation.1 | convolution fusion | flops 536870912 | bytes 5505024 | tf_op jit(solution)/shard_map/dot_general | solution.py:147
  20.1 0.8 fusion.19
  21.0 0.1 copy.27
  21.2 0.7 fusion.2
  21.9 0.1 fusion.16
  22.0 8.5 %all_to_all.31 = bf16[4,8,2,16,128]{4,3,2,1,0:T(8,128)(2,1)S(1)} all-to-all(bf16[4,8,2,16,128]{4,3,2,1,0:T(8,128)(2,1)S(1)} %bitcast.43), channel_id=1, replica_groups=mesh['sta'=64,'tm'=4] {'tm'}, dimensions={0} | all-to-all | bytes 524288 | tf_op jit(solution)/shard_map/all_to_all | solution.py:175
  30.6 0.7 copy.30
  31.3 0.0 all-gather.2.cloned.1.call-update
  31.3 0.1 copy.25
  31.4 0.1 reshape.91
  31.6 2.5 %sort.17 = (s32[128]{0:T(128)}, s32[128]{0:T(128)S(1)}) sort(s32[128]{0:T(128)S(1)} %and_select_fusion, s32[128]{0:T(128)S(1)} %iota.15), dimensions={0}, to_apply=%region_0.1 | sort | flops 896 | bytes 2048 | tf_op jit(solution)/shard_map/jit(argsort)/sort | solution.py:111
  34.1 1.2 gather_fusion
  35.4 0.1 convert_reduce_fusion
  35.5 0.2 reduce-window.9
  35.7 0.1 pad_add_fusion.bound_ref
  35.7 1.0 bitcast_convert_fusion.own_ref
  36.7 97.6 %all-gather.2.cloned.1.call-done.part_ref = bf16[64,8,128,128]{3,2,1,0:T(8,128)(2,1)} async-done(((bf16[1,8,128,128]{3,2,1,0:T(8,128)(2,1)}), bf16[64,8,128,128]{3,2,1,0:T(8,128)(2,1)}) %all-gather.2.cloned.1.call-update) | async-done | bytes 16777232 | tf_op jit(solution)/shard_map/all_gather | solution.py:178
  134.3 47.5 %shard_map.47 = bf16[64,2,128,128]{3,2,1,0:T(8,128)(2,1)} custom-call(s32[128]{0:T(128)S(1)} %get-tuple-element.6.order_ref, s32[128]{0:T(128)S(1)} %gather_fusion, s32[9]{0:T(128)S(1)} %pad_add_fusion.bound_ref, bf16[64,8,128,128]{3,2,1,0:T(8,128)(2,1)} %all-gather.2.cloned.1.call-done.part_ref, f32[8,128,128]{2,1,0:T(8,128)S(1)} %bitcast_convert_fusion.own_ref), custom_call_target="tpu_custom_call" | custom-call | tf_op jit(solution)/shard_map/pallas_call | solution.py:132
  (13 shorter events, 0.2 us)
Async XLA Ops:
  6.5 10.4 %all-to-all-start = ((bf16[4,16,2048]{2,1,0:T(8,128)(2,1)}), bf16[4,16,2048]{2,1,0:T(8,128)(2,1)S(1)}, u32[]{:S(2)}, u32[]{:S(2)}) async-start(bf16[4,16,2048]{2,1,0:T(8,128)(2,1)} %bitcast.45), calls=%async_computation | async-start | bytes 524288 | tf_op jit(solution)/shard_map/all_to_all | solution.py:143
  11.4 122.9 %all-gather.2.cloned.1.call-start = ((), (), s32[]{:S(2)}) async-start(), calls=%async_computation.2 | async-start | bytes 17039360 | tf_op jit(solution)/shard_map/all_gather | solution.py:178
  15.7 4.4 %copy-start = (bf16[4,2,128,1024]{3,2,1,0:T(8,128)(2,1)S(1)}, bf16[4,2,128,1024]{3,2,1,0:T(8,128)(2,1)}, u32[]{:S(2)}) copy-start(bf16[4,2,128,1024]{3,2,1,0:T(8,128)(2,1)} %constant.61) | copy-start | bytes 6291460
  21.2 10.2 %copy-start.1 = (s32[64,2]{0,1:T(2,128)S(1)}, s32[64,2]{0,1:T(2,128)}, u32[]{:S(2)}) copy-start(s32[64,2]{0,1:T(2,128)} %param.6) | copy-start | bytes 1540
Sparse Core Ops, SparseCore 0:
  31.4 102.8 all-gather.1

commit v11 on v10

--- a/solution.py
+++ b/solution.py
@@ -104,7 +104,7 @@
             pltpu.make_async_copy(scr.at[last % 2], out_hbm.at[0, 0], sem.at[last % 2]).wait()
 
 
-def correlate(owners, part, own, out_shape, n_parts=8):
+def correlate(owners, part, own, out_shape, n_parts=16):
     n_blocks, n_win, rows, freq = part.shape
     n_half = n_blocks // n_parts
     part_of = (owners // n_half).astype(jnp.int32)

time: 189 us -> 189 us (level)
  no operation moved by 1% of the time
where the time goes in v11:
time: 189 us; the launch traced here: 188 us
  waiting for transfers between devices  98.7 us (52%)
  Pallas kernels  50.2 us (27%)
  between operations  13.5 us (7%)
  blocking collectives  8.53 us (5%)
  other arithmetic  5.25 us (3%)
  starting transfers between devices  4.83 us (3%)
  matrix products  4.45 us (2%)
  local copies, waits for them, and re-layouts  2.79 us (1%)
    all_gather x1, waiting for transfers between devices, shards(): gathered = lax.all_gather(contribution, 'sta', axis=0, tiled=False)  97.5 us
    pallas_call x1, Pallas kernels, correlate(): pl.pallas_call(corr_kernel, out_shape=jax.ShapeDtypeStruct(out_shape, jnp...  47.1 us
    all_to_all x1, blocking collectives, shards(): lax.all_to_all(whitened, 'tm', split_axis=0, concat_axis=3, tiled=True)  8.53 us
    all_to_all x1, starting transfers between devices, shards(): lax.all_to_all(records, 'tm', split_axis=0, concat_axis=1, tiled=True)  4.83 us
  transfers between devices with their start and end apart: 2, of which 2 were waited for; matrix products, arithmetic and copies ran while one was open for 4% of the time, Pallas kernels for 2%

profile of v11, /device:TPU:1, one launch (start us, length us, event | category | flops | bytes accessed | tf_op | source)
XLA Modules:
  0.0 188.3 jit_solution(11540033203720538266)
XLA Ops:
  6.5 4.8 %all-to-all-start = ((bf16[4,16,2048]{2,1,0:T(8,128)(2,1)}), bf16[4,16,2048]{2,1,0:T(8,128)(2,1)S(1)}, u32[]{:S(2)}, u32[]{:S(2)}) async-start(bf16[4,16,2048]{2,1,0:T(8,128)(2,1)} %bitcast.44), calls=%async_computation | async-start | bytes 524288 | tf_op jit(solution)/shard_map/all_to_all | solution.py:143
  11.4 1.3 pad_convert_fusion
  12.6 3.1 %shard_map.46 = bf16[1024,2048]{1,0:T(8,128)(2,1)} custom-call(f32[1,2048]{1,0:T(1,128)} %bitcast.46), custom_call_target="tpu_custom_call" | custom-call | tf_op jit(solution)/shard_map/pallas_call | solution.py:31
  15.7 1.2 all-to-all-done
  16.9 0.2 copy.31
  17.1 0.1 reshape.94
  17.2 2.9 %convolution_bitcast_fusion = f32[16,8,2048]{2,1,0:T(8,128)S(1)} fusion(bf16[128,1024]{1,0:T(8,128)(2,1)S(1)} %reshape.94, bf16[1024,2048]{1,0:T(8,128)(2,1)} %shard_map.46), kind=kOutput, calls=%fused_computation.1 | convolution fusion | flops 536870912 | bytes 5505024 | tf_op jit(solution)/shard_map/dot_general | solution.py:147
  20.1 0.8 fusion.19
  21.0 0.1 copy.32
  21.2 0.7 fusion.2
  21.9 0.1 fusion.16
  22.0 8.5 %all_to_all.31 = bf16[4,8,2,16,128]{4,3,2,1,0:T(8,128)(2,1)S(1)} all-to-all(bf16[4,8,2,16,128]{4,3,2,1,0:T(8,128)(2,1)S(1)} %bitcast.42), channel_id=1, replica_groups=mesh['sta'=64,'tm'=4] {'tm'}, dimensions={0} | all-to-all | bytes 524288 | tf_op jit(solution)/shard_map/all_to_all | solution.py:175
  30.6 0.7 copy.35
  31.3 0.1 copy.29
  31.4 0.1 reshape.91
  31.6 2.5 %sort.17 = (s32[128]{0:T(128)}, s32[128]{0:T(128)S(1)}) sort(s32[128]{0:T(128)S(1)} %and_select_fusion, s32[128]{0:T(128)S(1)} %iota.15), dimensions={0}, to_apply=%region_0.1 | sort | flops 896 | bytes 2048 | tf_op jit(solution)/shard_map/jit(argsort)/sort | solution.py:111
  34.1 1.2 gather_fusion
  35.4 0.1 convert_reduce_fusion
  35.5 0.1 copy.30
  35.6 0.1 reduce
  35.7 0.1 pad_add_fusion.bound_ref
  35.8 1.0 bitcast_convert_fusion.own_ref
  36.8 97.5 %all-gather.2.cloned.1.call-done.part_ref = bf16[64,8,128,128]{3,2,1,0:T(8,128)(2,1)} async-done(((bf16[1,8,128,128]{3,2,1,0:T(8,128)(2,1)}), bf16[64,8,128,128]{3,2,1,0:T(8,128)(2,1)}) %all-gather.2.cloned.1.call-update) | async-done | bytes 16777232 | tf_op jit(solution)/shard_map/all_gather | solution.py:178
  134.3 47.1 %shard_map.47 = bf16[64,2,128,128]{3,2,1,0:T(8,128)(2,1)} custom-call(s32[128]{0:T(128)S(1)} %get-tuple-element.6.order_ref, s32[128]{0:T(128)S(1)} %gather_fusion, s32[17]{0:T(128)S(1)} %pad_add_fusion.bound_ref, bf16[64,8,128,128]{3,2,1,0:T(8,128)(2,1)} %all-gather.2.cloned.1.call-done.part_ref, f32[8,128,128]{2,1,0:T(8,128)S(1)} %bitcast_convert_fusion.own_ref), custom_call_target="tpu_custom_call" | custom-call | tf_op jit(solution)/shard_map/pallas_call | solution.py:132
  (15 shorter events, 0.2 us)
Async XLA Ops:
  6.5 10.4 %all-to-all-start = ((bf16[4,16,2048]{2,1,0:T(8,128)(2,1)}), bf16[4,16,2048]{2,1,0:T(8,128)(2,1)S(1)}, u32[]{:S(2)}, u32[]{:S(2)}) async-start(bf16[4,16,2048]{2,1,0:T(8,128)(2,1)} %bitcast.44), calls=%async_computation | async-start | bytes 524288 | tf_op jit(solution)/shard_map/all_to_all | solution.py:143
  11.4 122.9 %all-gather.2.cloned.1.call-start = ((), (), s32[]{:S(2)}) async-start(), calls=%async_computation.2 | async-start | bytes 17039360 | tf_op jit(solution)/shard_map/all_gather | solution.py:178
  15.7 4.4 %copy-start = (bf16[4,2,128,1024]{3,2,1,0:T(8,128)(2,1)S(1)}, bf16[4,2,128,1024]{3,2,1,0:T(8,128)(2,1)}, u32[]{:S(2)}) copy-start(bf16[4,2,128,1024]{3,2,1,0:T(8,128)(2,1)} %constant.61) | copy-start | bytes 6291460
  21.2 10.2 %copy-start.1 = (s32[64,2]{0,1:T(2,128)S(1)}, s32[64,2]{0,1:T(2,128)}, u32[]{:S(2)}) copy-start(s32[64,2]{0,1:T(2,128)} %param.6) | copy-start | bytes 1540
Sparse Core Ops, SparseCore 0:
  31.4 102.8 all-gather.1

commit v12 on v11

--- a/solution.py
+++ b/solution.py
@@ -62,11 +62,10 @@
 
 def corr_kernel(order_ref, blk_ref, bound_ref, part_ref, own_ref, out_hbm, scr, wide, sem):
     h = pl.program_id(0)
-    n_half, n_win, rows_all, freq = part_ref.shape
+    n_half, n_src, n_win, rows, freq = part_ref.shape
     n_pairs = order_ref.shape[0]
     n_top = out_hbm.shape[1]
-    half = rows_all // 2
-    chunk = min(ROWS, half)
+    per = rows // 2
 
     def one(i, carry):
         slot = i % 2
@@ -79,18 +78,18 @@
         def _():
             pltpu.make_async_copy(scr.at[slot], out_hbm.at[0, 0], sem.at[slot]).wait()
 
-        for c0 in range(0, half, chunk):
-            real_sum = jnp.zeros((chunk, freq), jnp.float32)
-            imag_sum = jnp.zeros((chunk, freq), jnp.float32)
+        for src in range(n_src):
+            real_sum = jnp.zeros((per, freq), jnp.float32)
+            imag_sum = jnp.zeros((per, freq), jnp.float32)
             for w in range(n_win):
-                par_re = part_ref[b, w, c0 : c0 + chunk, :].astype(jnp.float32)
-                par_im = part_ref[b, w, half + c0 : half + c0 + chunk, :].astype(jnp.float32)
-                sig_re = own_ref[w, pl.ds(s, 1), :]
-                sig_im = own_ref[w, pl.ds(half + s, 1), :]
+                par_re = part_ref[b, src, w, 0:per, :].astype(jnp.float32)
+                par_im = part_ref[b, src, w, per:rows, :].astype(jnp.float32)
+                sig_re = own_ref[s // per, w, pl.ds(s % per, 1), :]
+                sig_im = own_ref[s // per, w, pl.ds(per + s % per, 1), :]
                 real_sum = real_sum + par_re * sig_re + par_im * sig_im
                 imag_sum = imag_sum + par_re * sig_im - par_im * sig_re
-            wide[pl.ds(2 * c0, chunk, stride=2), :] = real_sum
-            wide[pl.ds(2 * c0 + 1, chunk, stride=2), :] = imag_sum
+            wide[pl.ds(2 * src * per, per, stride=2), :] = real_sum
+            wide[pl.ds(2 * src * per + 1, per, stride=2), :] = imag_sum
         scr[slot] = wide[...].astype(scr.dtype)
         pltpu.make_async_copy(scr.at[slot], out_hbm.at[s, k], sem.at[slot]).start()
         return carry
@@ -105,7 +104,7 @@
 
 
 def correlate(owners, part, own, out_shape, n_parts=16):
-    n_blocks, n_win, rows, freq = part.shape
+    n_blocks, n_src, n_win, rows, freq = part.shape
     n_half = n_blocks // n_parts
     part_of = (owners // n_half).astype(jnp.int32)
     order = jnp.argsort(part_of, stable=True).astype(jnp.int32)
@@ -119,13 +118,13 @@
         num_scalar_prefetch=3,
         grid=(n_parts,),
         in_specs=[
-            pl.BlockSpec((n_half, n_win, rows, freq), lambda h, *_: (h, 0, 0, 0)),
-            pl.BlockSpec(own.shape, lambda h, *_: (0, 0, 0)),
+            pl.BlockSpec((n_half, n_src, n_win, rows, freq), lambda h, *_: (h, 0, 0, 0, 0)),
+            pl.BlockSpec(own.shape, lambda h, *_: (0, 0, 0, 0)),
         ],
         out_specs=pl.BlockSpec(memory_space=pl.ANY),
         scratch_shapes=[
-            pltpu.VMEM((2, rows, freq), jnp.bfloat16),
-            pltpu.VMEM((rows, freq), jnp.float32),
+            pltpu.VMEM((2, n_src * rows, freq), jnp.bfloat16),
+            pltpu.VMEM((n_src * rows, freq), jnp.float32),
             pltpu.SemaphoreType.DMA((2,)),
         ],
     )
@@ -172,9 +171,9 @@
     whitened = whitened.reshape(station_count, NW, quarters, 2, per_quarter).transpose(
         2, 1, 3, 0, 4
     )
-    contribution = lax.all_to_all(whitened, "tm", split_axis=0, concat_axis=3, tiled=True)
-    own_count = contribution.shape[3]
-    contribution = contribution.reshape(NW, own_count * 2, per_quarter)
+    contribution = lax.all_to_all(whitened, "tm", split_axis=0, concat_axis=0, tiled=True)
+    own_count = quarters * station_count
+    contribution = contribution.reshape(quarters, NW, 2 * station_count, per_quarter)
     gathered = lax.all_gather(contribution, "sta", axis=0, tiled=False)
     own = contribution.astype(jnp.float32)
     out_shape = (own_count, station_owners.shape[1], own_count * 2, per_quarter)

time: 189 us -> 189 us (level)
  no operation moved by 1% of the time
where the time goes in v12:
time: 189 us; the launch traced here: 188 us
  waiting for transfers between devices  99.2 us (52%)
  Pallas kernels  50.3 us (27%)
  between operations  13.5 us (7%)
  blocking collectives  8.64 us (5%)
  other arithmetic  5.27 us (3%)
  starting transfers between devices  4.83 us (3%)
  matrix products  4.45 us (2%)
  local copies, waits for them, and re-layouts  2.06 us (1%)
    all_gather x1, waiting for transfers between devices, shards(): gathered = lax.all_gather(contribution, 'sta', axis=0, tiled=False)  98 us
    pallas_call x1, Pallas kernels, correlate(): pl.pallas_call(corr_kernel, out_shape=jax.ShapeDtypeStruct(out_shape, jnp...  47.3 us
    all_to_all x1, blocking collectives, shards(): lax.all_to_all(whitened, 'tm', split_axis=0, concat_axis=0, tiled=True)  8.64 us
    all_to_all x1, starting transfers between devices, shards(): lax.all_to_all(records, 'tm', split_axis=0, concat_axis=1, tiled=True)  4.83 us
  transfers between devices with their start and end apart: 2, of which 2 were waited for; matrix products, arithmetic and copies ran while one was open for 4% of the time, Pallas kernels for 2%

profile of v12, /device:TPU:1, one launch (start us, length us, event | category | flops | bytes accessed | tf_op | source)
XLA Modules:
  0.0 188.4 jit_solution(13699609942539075413)
XLA Ops:
  6.5 4.8 %all-to-all-start = ((bf16[4,16,2048]{2,1,0:T(8,128)(2,1)}), bf16[4,16,2048]{2,1,0:T(8,128)(2,1)S(1)}, u32[]{:S(2)}, u32[]{:S(2)}) async-start(bf16[4,16,2048]{2,1,0:T(8,128)(2,1)} %bitcast.39), calls=%async_computation | async-start | bytes 524288 | tf_op jit(solution)/shard_map/all_to_all | solution.py:142
  11.4 1.3 pad_convert_fusion
  12.6 3.1 %shard_map.46 = bf16[1024,2048]{1,0:T(8,128)(2,1)} custom-call(f32[1,2048]{1,0:T(1,128)} %bitcast.41), custom_call_target="tpu_custom_call" | custom-call | tf_op jit(solution)/shard_map/pallas_call | solution.py:31
  15.7 1.2 all-to-all-done
  16.9 0.2 copy.23
  17.1 0.1 reshape.92
  17.2 2.9 %convolution_bitcast_fusion = f32[16,8,2048]{2,1,0:T(8,128)S(1)} fusion(bf16[128,1024]{1,0:T(8,128)(2,1)S(1)} %reshape.92, bf16[1024,2048]{1,0:T(8,128)(2,1)} %shard_map.46), kind=kOutput, calls=%fused_computation.1 | convolution fusion | flops 536870912 | bytes 5505024 | tf_op jit(solution)/shard_map/dot_general | solution.py:146
  20.1 0.8 fusion.19
  21.0 0.1 copy.24
  21.2 0.7 fusion.2
  21.9 0.1 fusion.16
  22.0 8.6 %all_to_all.21 = bf16[4,8,2,16,128]{4,3,2,1,0:T(8,128)(2,1)} all-to-all(bf16[4,8,2,16,128]{4,3,2,1,0:T(8,128)(2,1)S(1)} %bitcast.37), channel_id=1, replica_groups=mesh['sta'=64,'tm'=4] {'tm'}, dimensions={0} | all-to-all | bytes 524288 | tf_op jit(solution)/shard_map/all_to_all | solution.py:174
  30.7 0.0 all-gather.2.cloned.1.call-update
  30.7 0.1 copy.21
  30.8 0.1 reshape.89
  31.0 2.5 %sort.17 = (s32[128]{0:T(128)}, s32[128]{0:T(128)S(1)}) sort(s32[128]{0:T(128)S(1)} %and_select_fusion, s32[128]{0:T(128)S(1)} %iota.15), dimensions={0}, to_apply=%region_0.1 | sort | flops 896 | bytes 2048 | tf_op jit(solution)/shard_map/jit(argsort)/sort | solution.py:110
  33.5 1.2 gather_fusion
  34.7 0.1 convert_reduce_fusion
  34.9 0.1 copy.22
  35.0 0.1 reduce
  35.1 0.1 pad_add_fusion.bound_ref
  35.2 1.0 bitcast_convert_fusion.own_ref
  36.2 98.0 %all-gather.2.cloned.1.call-done.part_ref = bf16[64,4,8,32,128]{4,3,2,1,0:T(8,128)(2,1)} async-done(((bf16[1,4,8,32,128]{4,3,2,1,0:T(8,128)(2,1)}), bf16[64,4,8,32,128]{4,3,2,1,0:T(8,128)(2,1)}) %all-gather.2.cloned.1.call-update) | async-done | bytes 16777232 | tf_op jit(solution)/shard_map/all_gather | solution.py:177
  134.2 47.3 %shard_map.47 = bf16[64,2,128,128]{3,2,1,0:T(8,128)(2,1)} custom-call(s32[128]{0:T(128)S(1)} %get-tuple-element.6.order_ref, s32[128]{0:T(128)S(1)} %gather_fusion, s32[17]{0:T(128)S(1)} %pad_add_fusion.bound_ref, bf16[64,4,8,32,128]{4,3,2,1,0:T(8,128)(2,1)} %all-gather.2.cloned.1.call-done.part_ref, f32[4,8,32,128]{3,2,1,0:T(8,128)S(1)} %bitcast_convert_fusion.own_ref), custom_call_target="tpu_custom_call" | custom-call | tf_op jit(solution)/shard_map/pallas_call | solution.py:131
  (14 shorter events, 0.2 us)
Async XLA Ops:
  6.5 10.4 %all-to-all-start = ((bf16[4,16,2048]{2,1,0:T(8,128)(2,1)}), bf16[4,16,2048]{2,1,0:T(8,128)(2,1)S(1)}, u32[]{:S(2)}, u32[]{:S(2)}) async-start(bf16[4,16,2048]{2,1,0:T(8,128)(2,1)} %bitcast.39), calls=%async_computation | async-start | bytes 524288 | tf_op jit(solution)/shard_map/all_to_all | solution.py:142
  11.4 122.9 %all-gather.2.cloned.1.call-start = ((), (), s32[]{:S(2)}) async-start(), calls=%async_computation.2 | async-start | bytes 17039360 | tf_op jit(solution)/shard_map/all_gather | solution.py:177
  15.7 4.4 %copy-start = (bf16[4,2,128,1024]{3,2,1,0:T(8,128)(2,1)S(1)}, bf16[4,2,128,1024]{3,2,1,0:T(8,128)(2,1)}, u32[]{:S(2)}) copy-start(bf16[4,2,128,1024]{3,2,1,0:T(8,128)(2,1)} %constant.61) | copy-start | bytes 6291460
  21.0 9.7 %copy-start.1 = (s32[64,2]{0,1:T(2,128)S(1)}, s32[64,2]{0,1:T(2,128)}, u32[]{:S(2)}) copy-start(s32[64,2]{0,1:T(2,128)} %param.6) | copy-start | bytes 1540
Sparse Core Ops, SparseCore 0:
  30.8 103.3 all-gather.1
